TPU v7x, 32 devices: a whole 2x2x4 slice. The times are simulated.
32 devices in a mesh: grp: 2 (over y), ctx: 4 (over z), tp: 4 (over x, core).
Axes of the slice: x: 2, y: 2, z: 4, core: 2. Of those that a mesh axis runs over, the one named last changes fastest.
Arguments:
- tokens: bfloat16 [3072, 4096], P(('grp', 'ctx'), 'tp'), parts along dimension 0, may hold values from -6 to 6
- norm_gain: bfloat16 [4096], P('tp'), may hold values from 0.099609375 to 1.8984375
- w_in: bfloat16 [4096, 3, 2048], P('ctx', None, 'tp'), may hold values from -0.09375 to 0.09375
- short_taps: float32 [3, 3, 2048], P(None, None, 'tp'), may hold values from -3.5 to 3.5
- rates: float32 [128, 64], P('tp'), may hold values from 6.510417e-06 to 0.03
- residues: float32 [128, 64], P('tp'), may hold values from -4 to 4
- w_out: bfloat16 [2048, 4096], P(None, 'tp'), may hold values from -0.125 to 0.125
Outputs:
- layer_out: bfloat16 [3072, 4096], P(('grp', 'ctx'), 'tp'), parts along dimension 0
There are 2 independent parts, one for each index of `grp`. A program takes and returns all parts, laid end to end along the dimension named above; an argument that names none is the same for every part. Nothing has to cross between parts.
All inputs are finite; a program needn't handle non-finite values.
Results may differ from a plain program's by a relative error of at most 0.0067.
Values may be sent and summed in bfloat16 or wider, within the bound.
No kernel may reach another device: no remote copies, remote signals or barrier semaphores. Data moves between devices by JAX's collectives and lax.ppermute only.
A program may use at most 128 MiB of HBM per device.

v0:
```python
import jax
import jax.numpy as jnp
from jax import lax
from jax.sharding import PartitionSpec as P

BLOCK = 128


def shifted(x, axis, by):
    count = lax.axis_size(axis)
    pairs = [(i, i + by) for i in range(count) if 0 <= i + by < count]
    return lax.ppermute(x, axis, pairs)


def short_filter(extended, taps, count):
    values = extended.astype(jnp.float32)
    result = jnp.zeros((count, values.shape[1]), jnp.float32)
    span = taps.shape[0]
    for tap_index in range(span):
        begin = span - 1 - tap_index
        result = result + taps[tap_index] * values[begin : begin + count]
    return result


def banded(series):
    group_count, length = series.shape
    padded = jnp.concatenate([series, jnp.zeros_like(series)], axis=1)
    tiled = jnp.tile(padded, (1, length))
    return tiled[:, : length * (2 * length - 1)].reshape(group_count, length, 2 * length - 1)


def body(tokens, norm_gain, w_in, short_taps, rates, residues, w_out):
    tok_rows = tokens.shape[0]
    local_width = w_in.shape[2]
    local_groups = rates.shape[0]
    group_size = local_width // local_groups
    block_rows = BLOCK
    reach = block_rows - 1
    mode_count = rates.shape[1]
    highest = lax.Precision.HIGHEST
    gathered, gain_whole = (
        lax.all_gather(tokens, "tp", axis=1, tiled=True),
        lax.all_gather(norm_gain, "tp", axis=0, tiled=True),
    )
    values = gathered.astype(jnp.float32)
    scale = lax.rsqrt(jnp.mean(values * values, axis=1, keepdims=True) + 1e-06)
    normed = (values * scale * gain_whole.astype(jnp.float32)).astype(jnp.bfloat16)
    shards = lax.all_gather(w_in, "ctx", axis=0, tiled=True)
    flat = shards.reshape(shards.shape[0], 3 * local_width)
    summed = jnp.dot(normed, flat, preferred_element_type=jnp.float32)
    projected = summed.astype(jnp.bfloat16)
    span = short_taps.shape[0]
    taps = short_taps.reshape(span, 3 * local_width)
    before = shifted(projected[tok_rows - (span - 1) :], "ctx", 1)
    filtered = short_filter(jnp.concatenate([before, projected], axis=0), taps, tok_rows)
    product = filtered[:, :local_width] * filtered[:, 2 * local_width :]
    second = filtered[:, local_width : 2 * local_width]
    decay = rates[:, :, None]
    coef = residues * jnp.sqrt(-jnp.expm1(-2.0 * rates)) * mode_count ** (-0.5)
    lags = jnp.arange(block_rows).astype(jnp.float32)
    powers = jnp.exp(-decay * lags)
    long_taps = jnp.einsum("gn,gnt->gt", coef, powers, precision=highest)
    kernel = banded(long_taps[:, ::-1])[:, :, reach:]
    blocks = tok_rows // block_rows
    current = product.reshape(blocks, block_rows, local_groups, group_size)
    near = jnp.einsum("gij,bjgc->bigc", kernel, current, precision=highest)
    tail = jnp.exp(-decay * (reach - lags))
    ends = jnp.einsum("gni,bigc->bgnc", tail, current, precision=highest)
    step_decay = jnp.exp(-decay * block_rows)

    def advance(state, end_block):
        return (step_decay * state + end_block, state)

    zero_state = jnp.zeros((local_groups, mode_count, group_size), jnp.float32)
    own_state, local_starts = lax.scan(advance, zero_state, ends)
    position = lax.axis_index("ctx")
    shards = lax.all_gather(own_state[None], "ctx", axis=0, tiled=True)
    source = jnp.arange(shards.shape[0])
    distance = (position - 1 - source).astype(jnp.float32)[:, None, None]
    weight = jnp.where(
        distance >= 0.0, jnp.exp(-rates[None] * tok_rows * jnp.maximum(distance, 0.0)), 0.0
    )
    incoming = jnp.einsum("kgn,kgnc->gnc", weight, shards, precision=highest)
    block_index = jnp.arange(blocks).astype(jnp.float32)
    lead = jnp.exp(-decay[None] * block_rows * block_index[:, None, None, None])
    starts = lead * incoming[None] + local_starts
    entry = coef[:, None, :] * jnp.exp(-rates[:, None, :] * (lags[None, :, None] + 1.0))
    distant = jnp.einsum("gin,bgnc->bigc", entry, starts, precision=highest)
    conv_out = (near + distant).reshape(tok_rows, local_width)
    gated = (second * conv_out).astype(jnp.bfloat16)
    mixed = jnp.dot(
        lax.all_gather(gated, "tp", axis=1, tiled=True), w_out, preferred_element_type=jnp.float32
    )
    return (tokens.astype(jnp.float32) + mixed).astype(jnp.bfloat16)


def solution(mesh):
    in_specs = (
        P(("grp", "ctx"), "tp"),
        P("tp"),
        P("ctx", None, "tp"),
        P(None, None, "tp"),
        P("tp", None),
        P("tp", None),
        P(None, "tp"),
    )
    out_specs = P(("grp", "ctx"), "tp")
    return jax.shard_map(body, mesh=mesh, in_specs=in_specs, out_specs=out_specs, check_vma=False)
```

profile of v0, /device:TPU:0, one launch (start us, length us, event | category | flops | bytes accessed | tf_op | source)
XLA Modules:
  0.0 359.3 jit_solution(6902733340890311691)
XLA Ops:
  6.5 0.7 all-gather.5.cloned.1.call-update
  7.3 4.7 %copy.21 = bf16[1024,3,512]{0,2,1:T(8,128)(2,1)} copy(bf16[1024,3,512]{2,0,1:T(8,128)(2,1)} %param.11) | data formatting | bytes 6291456 | tf_op args[2]
  12.1 0.6 copy-done.8
  12.7 6.2 %all_gather.16 = bf16[4096]{0:T(1024)(128)(2,1)S(1)} all-gather(bf16[1024]{0:T(1024)(128)(2,1)S(1)} %copy-done.8), channel_id=1, replica_groups=mesh['grp'=2,'ctx'=4,'tp'=4] {'tp'}, dimensions={0}, use_global_device_ids=true | all-gather | bytes 10240 | tf_op jit(solution)/shard_map/all_gather | solution.py:43
  18.8 0.5 broadcast_add_fusion
  19.4 1.1 fusion.23
  20.8 19.4 %all-gather.5.cloned.1.call-done = bf16[384,4096]{1,0:T(8,128)(2,1)} async-done(((bf16[384,1024]{1,0:T(8,128)(2,1)}), bf16[384,4096]{1,0:T(8,128)(2,1)}) %all-gather.5.cloned.1.call-update) | async-done | bytes 3145744 | tf_op jit(solution)/shard_map/all_gather | solution.py:42
  40.2 2.7 fusion
  42.9 217.0 %all-gather.7.cloned.1.call-done = bf16[4096,3,512]{0,2,1:T(8,128)(2,1)} async-done(((bf16[1024,3,512]{0,2,1:T(8,128)(2,1)}), bf16[4096,3,512]{0,2,1:T(8,128)(2,1)}) %all-gather.7.cloned.1.call-update) | async-done | bytes 12582928 | tf_op jit(solution)/shard_map/all_gather | solution.py:48
  259.9 8.2 %fusion.7 = bf16[384,1536]{1,0:T(8,128)(2,1)S(1)} fusion(bf16[4096,1536]{0,1:T(8,128)(2,1)} %bitcast.72, bf16[384,4096]{1,0:T(8,128)(2,1)S(1)} %copy-done.1, f32[4096]{0:T(1024)S(1)} %convert_element_type.61, f32[384]{0:T(512)S(1)} %add_rsqrt_fusion), kind=kOutput, calls=%fused_computation.10 | convolution fusion | flops 4838719488 | bytes 16926208 | tf_op jit(solution)/shard_map/dot_general | solution.py:50
  268.2 1.5 collective-permute-start
  269.7 0.5 broadcast_subtract_fusion
  270.7 2.4 copy.43
  273.1 2.2 slice.58
  275.4 9.5 %reshape.84 = f32[32,128,255]{2,1,0:T(8,128)} reshape(f32[32,32640]{1,0:T(8,128)} %slice.58) | data formatting | bytes 8355840 | tf_op jit(solution)/shard_map/reshape | solution.py:29
  285.2 0.7 fusion.10
  285.9 1.0 slice_multiply_fusion.3
  286.9 1.4 copy.22
  288.4 1.3 reshape.83
  289.6 3.1 convolution_bitcast_fusion
  292.7 2.6 while.13
  292.7 0.7 bitcast_dynamic-update-slice_fusion.2
  293.6 0.7 bitcast_dynamic-update-slice_fusion.2
  294.4 0.7 bitcast_dynamic-update-slice_fusion.2
  295.3 21.9 %all-gather = f32[128,64,16]{1,2,0:T(8,128)S(1)} all-gather(f32[32,64,16]{1,2,0:T(8,128)S(1)} %get-tuple-element.33), channel_id=2, replica_groups=mesh['grp'=2,'ctx'=4,'tp'=4] {'ctx'}, dimensions={0}, use_global_device_ids=true | all-gather | bytes 655360 | tf_op jit(solution)/shard_map/all_gather | solution.py:77
  317.3 2.7 fusion.15
  320.1 4.7 %fusion.14 = f32[3,128,32,16]{1,3,0,2:T(8,128)S(1)} fusion(f32[32,3,16,128]{3,2,1,0:T(8,128)S(1)} %fusion.15, f32[32,128,255]{2,1,0:T(8,128)S(1)} %copy-done, f32[3,128,32,16]{1,0,3,2:T(4,128)} %reshape.83), kind=kOutput, calls=%fused_computation.20 | convolution fusion | flops 302186496 | bytes 4456448 | tf_op jit(solution)/shard_map/gij,bjgc->bigc/dot_general | solution.py:66
  324.7 0.4 copy.27
  325.2 1.1 copy.28
  326.4 2.0 fusion.26
  328.4 18.9 %all-gather.9.cloned.1.call-done = bf16[384,2048]{1,0:T(8,128)(2,1)} async-done(((bf16[384,512]{1,0:T(8,128)(2,1)}), bf16[384,2048]{1,0:T(8,128)(2,1)}) %all-gather.9.cloned.1.call-update) | async-done | bytes 1572880 | tf_op jit(solution)/shard_map/all_gather | solution.py:92
  347.3 5.5 %add_convert_fusion = bf16[384,1024]{1,0:T(8,128)(2,1)} fusion(bf16[384,1024]{1,0:T(8,128)(2,1)} %param.9, bf16[384,2048]{1,0:T(8,128)(2,1)} %all-gather.9.cloned.1.call-done, bf16[2048,1024]{1,0:T(8,128)(2,1)} %param.15), kind=kOutput, calls=%fused_computation.18 | convolution fusion | flops 1611792384 | bytes 7340032 | tf_op jit(solution)/shard_map/dot_general | solution.py:91
  (48 shorter events, 1.7 us)
Async XLA Ops:
  6.5 33.6 %all-gather.5.cloned.1.call-start = ((), (), s32[]{:S(2)}) async-start(), calls=%async_computation | async-start | bytes 3932160 | tf_op jit(solution)/shard_map/all_gather | solution.py:42
  7.3 252.7 %all-gather.7.cloned.1.call-start = ((), (), s32[]{:S(2)}) async-start(), calls=%async_computation.1 | async-start | bytes 15728640 | tf_op jit(solution)/shard_map/all_gather | solution.py:48
  12.0 0.7 copy-start.8
  12.0 7.4 %copy-start.5 = (f32[3,3,512]{2,1,0:T(4,128)S(1)}, f32[3,3,512]{2,1,0:T(4,128)}, u32[]{:S(2)}) copy-start(f32[3,3,512]{2,1,0:T(4,128)} %param.12) | copy-start | bytes 55300
  12.0 7.4 %copy-start.6 = (f32[32,64]{1,0:T(8,128)S(1)}, f32[32,64]{1,0:T(8,128)}, u32[]{:S(2)}) copy-start(f32[32,64]{1,0:T(8,128)} %param.14) | copy-start | bytes 24580
  12.0 7.4 %copy-start.7 = (f32[32,64]{1,0:T(8,128)S(1)}, f32[32,64]{1,0:T(8,128)}, u32[]{:S(2)}) copy-start(f32[32,64]{1,0:T(8,128)} %param.13) | copy-start | bytes 24580
  12.0 335.3 %all-gather.9.cloned.1.call-start = ((), (), s32[]{:S(2)}) async-start(), calls=%async_computation.2 | async-start | bytes 1966080 | tf_op jit(solution)/shard_map/all_gather | solution.py:92
  19.4 1.2 copy-start.4
  40.2 219.8 %copy-start.1 = (bf16[384,4096]{1,0:T(8,128)(2,1)S(1)}, bf16[384,4096]{1,0:T(8,128)(2,1)}, u32[]{:S(2)}) copy-start(bf16[384,4096]{1,0:T(8,128)(2,1)} %all-gather.5.cloned.1.call-done) | copy-start | bytes 9437188
  268.2 1.5 copy-start.2
  268.2 16.7 %collective-permute-start = (bf16[2,1536]{1,0:T(2,128)(2,1)S(1)}, bf16[2,1536]{1,0:T(2,128)(2,1)S(1)}, u32[]{:S(2)}, u32[]{:S(2)}) collective-permute-start(bf16[2,1536]{1,0:T(2,128)(2,1)S(1)} %slice.51), channel_id=1, source_target_pairs={{0,4},{4,8},{8,12},{1,5},{5,9},{9,13},{2,6},{6,10},{10,14},{3,7},{... | collective-permute-start | bytes 18440 | tf_op jit(solution)/shard_map/ppermute | solution.py:12
  275.4 9.5 %copy-start.3 = (bf16[384,1536]{1,0:T(8,128)(2,1)S(1)}, bf16[384,1536]{1,0:T(8,128)(2,1)}, u32[]{:S(2)}) copy-start(bf16[384,1536]{1,0:T(8,128)(2,1)} %copy-done.2) | copy-start | bytes 3538948
  295.3 24.8 %copy-start = (f32[32,128,255]{2,1,0:T(8,128)S(1)}, f32[32,128,255]{2,1,0:T(8,128)}, u32[]{:S(2)}) copy-start(f32[32,128,255]{2,1,0:T(8,128)} %reshape.84) | copy-start | bytes 12533764
Sparse Core Ops, SparseCore 0:
  8.9 31.2 all-gather.4
  41.7 218.1 all-gather.6
  328.5 18.7 all-gather.8
where the time goes:
time: 360 us; the launch traced here: 359 us
  waiting for transfers between devices  256 us (71%)
  blocking collectives  28 us (8%)
  matrix products  25.3 us (7%)
  local copies, waits for them, and re-layouts  24.2 us (7%)
  between operations  13.3 us (4%)
  other arithmetic  10.7 us (3%)
    all_gather x1, waiting for transfers between devices, body(): shards = lax.all_gather(w_in, 'ctx', axis=0, tiled=True)  217 us
    all_gather x1, blocking collectives, body(): shards = lax.all_gather(own_state[None], 'ctx', axis=0, tiled=True)  21.9 us
    all_gather x1, waiting for transfers between devices, body(): lax.all_gather(tokens, 'tp', axis=1, tiled=True)  19.4 us
    all_gather x1, waiting for transfers between devices, body(): lax.all_gather(gated, 'tp', axis=1, tiled=True)  18.9 us
    reshape x1, local copies, waits for them, and re-layouts, banded(): tiled[:, :length * (2 * length - 1)]  9.51 us
    dot_general x1, matrix products, body(): summed = jnp.dot(normed, flat, preferred_element_type=jnp.float32)  8.23 us
    unnamed x21, local copies, waits for them, and re-layouts  7.79 us
  transfers between devices with their start and end apart: 4, of which 3 were waited for; matrix products, arithmetic and copies ran while one was open for 7% of the time, Pallas kernels for 0%

commit v1 on v0

--- a/solution.py
+++ b/solution.py
@@ -29,6 +29,17 @@
     return tiled[:, : length * (2 * length - 1)].reshape(group_count, length, 2 * length - 1)
 
 
+def gather_by_permutes(x, axis):
+    count = lax.axis_size(axis)
+    me = lax.axis_index(axis)
+    pieces = [x]
+    for by in range(1, count):
+        pairs = [(s, (s + by) % count) for s in range(count)]
+        pieces.append(lax.ppermute(x, axis, pairs))
+    stacked = jnp.stack(pieces[::-1], axis=0)
+    return jnp.roll(stacked, me + 1, axis=0)
+
+
 def body(tokens, norm_gain, w_in, short_taps, rates, residues, w_out):
     tok_rows = tokens.shape[0]
     local_width = w_in.shape[2]
@@ -38,17 +49,52 @@
     reach = block_rows - 1
     mode_count = rates.shape[1]
     highest = lax.Precision.HIGHEST
-    gathered, gain_whole = (
-        lax.all_gather(tokens, "tp", axis=1, tiled=True),
-        lax.all_gather(norm_gain, "tp", axis=0, tiled=True),
-    )
-    values = gathered.astype(jnp.float32)
+    n_ctx = lax.axis_size("ctx")
+    n_grp = lax.axis_size("grp")
+    me_ctx = lax.axis_index("ctx")
+    me_grp = lax.axis_index("grp")
+    shard_rows = w_in.shape[0]
+    piece = shard_rows // n_grp
+    streams = w_in.shape[1]
+
+    own = lax.dynamic_slice_in_dim(w_in, me_grp * piece, piece, axis=0)
+    relayed = []
+    for s in range(streams):
+        got = lax.all_gather(own[:, s, :], "ctx", axis=0)
+        doubled = jnp.concatenate([got, got], axis=0)
+        send = lax.dynamic_slice_in_dim(doubled, me_ctx + 1, n_ctx - 1, axis=0)
+        received = []
+        for by in range(1, n_grp):
+            pairs = [(q, (q + by) % n_grp) for q in range(n_grp)]
+            received.append(lax.ppermute(send, "grp", pairs))
+        relayed.append((got, received))
+
+    with_gain = jnp.concatenate([tokens, norm_gain[None]], axis=0)
+    stacked = gather_by_permutes(with_gain, "tp")
+    gathered = jnp.concatenate(list(stacked), axis=1)
+    values = gathered[:tok_rows].astype(jnp.float32)
+    gain_whole = gathered[tok_rows]
     scale = lax.rsqrt(jnp.mean(values * values, axis=1, keepdims=True) + 1e-06)
     normed = (values * scale * gain_whole.astype(jnp.float32)).astype(jnp.bfloat16)
-    shards = lax.all_gather(w_in, "ctx", axis=0, tiled=True)
-    flat = shards.reshape(shards.shape[0], 3 * local_width)
-    summed = jnp.dot(normed, flat, preferred_element_type=jnp.float32)
-    projected = summed.astype(jnp.bfloat16)
+    normed4 = normed.reshape(tok_rows, n_ctx, n_grp, piece)
+    mine = lax.dynamic_index_in_dim(normed4, me_grp, axis=2, keepdims=False)
+    others = []
+    for by in range(1, n_grp):
+        src_grp = (me_grp - by) % n_grp
+        part = lax.dynamic_index_in_dim(normed4, src_grp, axis=2, keepdims=False)
+        others.append((src_grp, jnp.roll(part, -me_ctx, axis=1)))
+    outputs = []
+    for s in range(streams):
+        got, received = relayed[s]
+        acc = jnp.einsum("tkr,krc->tc", mine, got, preferred_element_type=jnp.float32)
+        for (src_grp, part), recv in zip(others, received):
+            local = lax.dynamic_slice_in_dim(w_in[:, s, :], src_grp * piece, piece, axis=0)
+            acc = acc + jnp.dot(part[:, 0], local, preferred_element_type=jnp.float32)
+            acc = acc + jnp.einsum(
+                "tkr,krc->tc", part[:, 1:], recv, preferred_element_type=jnp.float32
+            )
+        outputs.append(acc)
+    projected = jnp.concatenate(outputs, axis=1).astype(jnp.bfloat16)
     span = short_taps.shape[0]
     taps = short_taps.reshape(span, 3 * local_width)
     before = shifted(projected[tok_rows - (span - 1) :], "ctx", 1)

time: 360 us -> 280 us (0.78)
  waiting for transfers between devices: 256 us -> 142 us
  local copies, waits for them, and re-layouts: 24.2 us -> 41.9 us
  other arithmetic: 10.7 us -> 21.6 us
  starting transfers between devices: 1.55 us -> 9.7 us
  blocking collectives: 28 us -> 21 us
  matrix products: 25.3 us -> 29.8 us
    all_gather x2 -> x3, waiting for transfers between devices: 236 us -> 66.9 us  [body(): got = lax.all_gather(own[:, s, :], 'ctx', axis=0)]
    ppermute x0 -> x6, waiting for transfers between devices: none -> 55.1 us  [the longest x3 28.6 us: gather_by_permutes(): pieces.append(lax.ppermute(x, axis, pairs))]
    concatenate x0 -> x6, other arithmetic: none -> 10.2 us  [the longest x3 8.73 us: body(): doubled = jnp.concatenate([got, got], axis=0)]
    dynamic_slice x0 -> x1, local copies, waits for them, and re-layouts: none -> 8.11 us  [body(): part = lax.dynamic_index_in_dim(normed4, src_grp, axis=2, keepdims=False)]
    ppermute x0 -> x6, starting transfers between devices: none -> 7.89 us  [the longest x3 4.64 us: body(): received.append(lax.ppermute(send, 'grp', pairs))]
    slice x1 -> x2, local copies, waits for them, and re-layouts: 0.01 us -> 6.22 us  [the longest x1 3.6 us: body(): w_in[:, s, :]]
    all_gather x1 -> x0, blocking collectives: 6.15 us -> none  [body(): lax.all_gather(norm_gain, 'tp', axis=0, tiled=True)]
    reshape x0 -> x1, local copies, waits for them, and re-layouts: none -> 4.94 us  [body(): normed4 = normed.reshape(tok_rows, n_ctx, n_grp, piece)]
  transfers between devices with their start and end apart: 4 -> 11, of which waited for: 3 -> 6; matrix products, arithmetic and copies ran while one was open for 7% -> 22% of each run, Pallas kernels for 0% -> 0%
where the time goes in v1:
time: 280 us
  waiting for transfers between devices  142 us (51%)
  local copies, waits for them, and re-layouts  41.9 us (15%)
  matrix products  29.8 us (11%)
  other arithmetic  21.6 us (8%)
  blocking collectives  21 us (8%)
  between operations  13.6 us (5%)
  starting transfers between devices  9.7 us (3%)
    all_gather x3, waiting for transfers between devices, body(): got = lax.all_gather(own[:, s, :], 'ctx', axis=0)  66.9 us
    ppermute x3, waiting for transfers between devices, gather_by_permutes(): pieces.append(lax.ppermute(x, axis, pairs))  28.6 us
    ppermute x3, waiting for transfers between devices, body(): received.append(lax.ppermute(send, 'grp', pairs))  26.6 us
    all_gather x1, blocking collectives, body(): shards = lax.all_gather(own_state[None], 'ctx', axis=0, tiled=True)  21 us
    all_gather x1, waiting for transfers between devices, body(): lax.all_gather(gated, 'tp', axis=1, tiled=True)  19.1 us
    reshape x1, local copies, waits for them, and re-layouts, banded(): tiled[:, :length * (2 * length - 1)]  9.41 us
    concatenate x3, other arithmetic, body(): doubled = jnp.concatenate([got, got], axis=0)  8.73 us
    dynamic_slice x1, local copies, waits for them, and re-layouts, body(): part = lax.dynamic_index_in_dim(normed4, src_grp, axis=2, keepdims=False)  8.11 us
  transfers between devices with their start and end apart: 11, of which 6 were waited for; matrix products, arithmetic and copies ran while one was open for 22% of the time, Pallas kernels for 0%

profile of v1, /device:TPU:0, one launch (start us, length us, event | category | flops | bytes accessed | tf_op | source)
XLA Modules:
  0.0 279.7 jit_solution(16622207129125613858)
XLA Ops:
  6.5 2.6 constant_dynamic-slice_fusion
  10.1 2.5 collective-permute-start
  13.4 3.6 %fusion.49 = (bf16[1024,1,512]{2,0,1:T(8,128)(2,1)}, bf16[1024,1,512]{2,0,1:T(8,128)(2,1)}, bf16[1024,1,512]{2,0,1:T(8,128)(2,1)}) fusion(bf16[1024,3,512]{2,0,1:T(8,128)(2,1)} %param.11), kind=kLoop, calls=%fused_computation.122 | loop fusion | bytes 6291456 | tf_op jit(solution)/shard_map/slice | solution.py:91
  17.8 1.7 fusion.26
  20.2 10.5 %collective-permute-done = bf16[385,1024]{1,0:T(8,128)(2,1)S(1)} collective-permute-done((bf16[385,1024]{1,0:T(8,128)(2,1)S(1)}, bf16[385,1024]{1,0:T(8,128)(2,1)S(1)}, u32[]{:S(2)}, u32[]{:S(2)}) %collective-permute-start) | collective-permute-done | bytes 788512 | tf_op jit(solution)/shard_map/ppermute | solution.py:38
  30.8 18.1 %collective-permute-done.1 = bf16[385,1024]{1,0:T(8,128)(2,1)S(1)} collective-permute-done((bf16[385,1024]{1,0:T(8,128)(2,1)S(1)}, bf16[385,1024]{1,0:T(8,128)(2,1)S(1)}, u32[]{:S(2)}, u32[]{:S(2)}) %collective-permute-start.1) | collective-permute-done | bytes 788512 | tf_op jit(solution)/shard_map/ppermute | solution.py:38
  51.4 2.7 fusion.2
  54.1 4.9 %reshape.84 = bf16[384,4,2,512]{3,2,1,0:T(2,128)(2,1)S(1)} reshape(bf16[384,4096]{1,0:T(8,128)(2,1)} %fusion.2) | data formatting | bytes 6291456 | tf_op jit(solution)/shard_map/reshape | solution.py:79
  59.0 8.1 %constant_dynamic-slice_fusion.2 = (bf16[384,4,1,512]{3,2,1,0:T(2,128)(2,1)S(1)}, bf16[384,4,1,512]{3,2,1,0:T(2,128)(2,1)}) fusion(bf16[384,4,2,512]{3,2,1,0:T(2,128)(2,1)S(1)} %reshape.84, s32[]{:T(128)S(6)} %select_n.58, s32[]{:T(128)S(6)} %select_n.55), kind=kLoop, calls=%fused_computation.111 | loop fusion | bytes 6291464 | tf_op jit(solution)/shard_map/jit(dynamic_index_in_dim)/dynamic_slice | solution.py:84
  68.6 3.1 %fusion.9 = bf16[3,512,512]{2,1,0:T(8,128)(2,1)} fusion(s32[]{:T(128)S(6)} %select_n.62, bf16[4,512,512]{2,1,0:T(8,128)(2,1)} %bitcast.147), kind=kLoop, calls=%fused_computation.26 | loop fusion | flops 786432 | bytes 3670020 | tf_op jit(solution)/shard_map/concatenate | solution.py:64
  71.7 1.6 collective-permute-start.3
  73.4 30.4 %all-gather.13.cloned.1.call-done = bf16[2048,1,512]{2,0,1:T(8,128)(2,1)} async-done(((bf16[512,1,512]{2,0,1:T(8,128)(2,1)}), bf16[2048,1,512]{2,0,1:T(8,128)(2,1)}) %all-gather.13.cloned.1.call-update) | async-done | bytes 2097168 | tf_op jit(solution)/shard_map/all_gather | solution.py:63
  103.8 3.3 %fusion.8 = bf16[3,512,512]{2,1,0:T(8,128)(2,1)} fusion(s32[]{:T(128)S(6)} %select_n.62, bf16[4,512,512]{2,1,0:T(8,128)(2,1)} %bitcast.149), kind=kLoop, calls=%fused_computation.25 | loop fusion | flops 786432 | bytes 3670020 | tf_op jit(solution)/shard_map/concatenate | solution.py:64
  108.5 3.7 %convolution_bitcast_fusion.5 = f32[384,512]{1,0:T(8,128)} fusion(bf16[4,512,512]{2,1,0:T(8,128)(2,1)} %bitcast.148, bf16[384,4,1,512]{3,2,1,0:T(2,128)(2,1)S(1)} %copy-done.1), kind=kOutput, calls=%fused_computation.37 | convolution fusion | flops 805306368 | bytes 4456448 | tf_op jit(solution)/shard_map/tkr,krc->tc/dot_general | solution.py:89
  113.3 36.5 %all-gather.15.cloned.1.call-done = bf16[2048,1,512]{2,0,1:T(8,128)(2,1)} async-done(((bf16[512,1,512]{2,0,1:T(8,128)(2,1)}), bf16[2048,1,512]{2,0,1:T(8,128)(2,1)}) %all-gather.15.cloned.1.call-update) | async-done | bytes 2097168 | tf_op jit(solution)/shard_map/all_gather | solution.py:63
  149.9 2.3 fusion.7
  152.2 1.5 collective-permute-start.5
  157.2 2.2 fusion.17
  159.4 2.2 fusion.16
  161.7 26.6 %collective-permute-done.5 = bf16[3,512,512]{2,1,0:T(8,128)(2,1)S(1)} collective-permute-done((bf16[3,512,512]{2,1,0:T(8,128)(2,1)S(1)}, bf16[3,512,512]{2,1,0:T(8,128)(2,1)S(1)}, u32[]{:S(2)}, u32[]{:S(2)}) %collective-permute-start.5) | collective-permute-done | bytes 1572896 | tf_op jit(solution)/shard_map/ppermute | solution.py:69
  189.0 1.7 collective-permute-start.6
  191.7 2.4 copy.49
  194.2 2.3 slice.103
  196.5 9.4 %reshape.86 = f32[32,128,255]{2,1,0:T(8,128)} reshape(f32[32,32640]{1,0:T(8,128)} %slice.103) | data formatting | bytes 8355840 | tf_op jit(solution)/shard_map/reshape | solution.py:29
  210.7 3.1 %convolution_bitcast_fusion.6 = f32[3,32,64,16]{2,3,0,1:T(8,128)S(1)} fusion(f32[3,128,32,16]{1,0,3,2:T(4,128)} %reshape.85, f32[128]{0:T(128)} %broadcast_subtract_fusion, f32[32,64]{1,0:T(8,128)S(1)} %get-tuple-element.97), kind=kOutput, calls=%fused_computation.41 | convolution fusion | flops 151257088 | bytes 1188352 | tf_op jit(solution)/shard_map/gni,bigc->bgnc/dot_general | solution.py:114
  213.7 2.6 while.13
  216.3 21.0 %all-gather.3 = f32[128,64,16]{1,2,0:T(8,128)S(1)} all-gather(f32[32,64,16]{1,2,0:T(8,128)S(1)} %get-tuple-element.33), channel_id=5, replica_groups=mesh['grp'=2,'ctx'=4,'tp'=4] {'ctx'}, dimensions={0}, use_global_device_ids=true | all-gather | bytes 655360 | tf_op jit(solution)/shard_map/all_gather | solution.py:123
  237.5 2.7 fusion.18
  240.2 4.7 %fusion.11 = f32[3,128,32,16]{1,3,0,2:T(8,128)S(1)} fusion(f32[32,3,16,128]{3,2,1,0:T(8,128)S(1)} %fusion.18, f32[32,128,255]{2,1,0:T(8,128)S(1)} %copy-done, f32[3,128,32,16]{1,0,3,2:T(4,128)} %reshape.85), kind=kOutput, calls=%fused_computation.31 | convolution fusion | flops 302186496 | bytes 4456448 | tf_op jit(solution)/shard_map/gij,bjgc->bigc/dot_general | solution.py:112
  246.5 2.0 fusion.29
  248.5 19.1 %all-gather.9.cloned.1.call-done = bf16[384,2048]{1,0:T(8,128)(2,1)} async-done(((bf16[384,512]{1,0:T(8,128)(2,1)}), bf16[384,2048]{1,0:T(8,128)(2,1)}) %all-gather.9.cloned.1.call-update) | async-done | bytes 1572880 | tf_op jit(solution)/shard_map/all_gather | solution.py:138
  267.6 5.5 %add_convert_fusion = bf16[384,1024]{1,0:T(8,128)(2,1)} fusion(bf16[384,1024]{1,0:T(8,128)(2,1)} %param.9, bf16[384,2048]{1,0:T(8,128)(2,1)} %all-gather.9.cloned.1.call-done, bf16[2048,1024]{1,0:T(8,128)(2,1)} %param.15), kind=kOutput, calls=%fused_computation.29 | convolution fusion | flops 1611792384 | bytes 7340032 | tf_op jit(solution)/shard_map/dot_general | solution.py:137
  (111 shorter events, 24.0 us)
Async XLA Ops:
  6.5 3.4 %copy-start.8 = (bf16[384,1024]{1,0:T(8,128)(2,1)S(1)}, bf16[384,1024]{1,0:T(8,128)(2,1)}, u32[]{:S(2)}) copy-start(bf16[384,1024]{1,0:T(8,128)(2,1)} %param.9) | copy-start | bytes 2359300
  6.5 62.1 %all-gather.11.cloned.1.call-start = ((), (), s32[]{:S(2)}) async-start(), calls=%async_computation.1 | async-start | bytes 2621440 | tf_op jit(solution)/shard_map/all_gather | solution.py:63
  6.5 3.5 %copy-start.18 = (bf16[1024]{0:T(1024)(128)(2,1)S(1)}, bf16[1024]{0:T(1024)(128)(2,1)}, u32[]{:S(2)}) copy-start(bf16[1024]{0:T(1024)(128)(2,1)} %param.10) | copy-start | bytes 6148
  9.2 94.6 %all-gather.13.cloned.1.call-start = ((), (), s32[]{:S(2)}) async-start(), calls=%async_computation.2 | async-start | bytes 2621440 | tf_op jit(solution)/shard_map/all_gather | solution.py:63
  9.9 139.9 %all-gather.15.cloned.1.call-start = ((), (), s32[]{:S(2)}) async-start(), calls=%async_computation.3 | async-start | bytes 2621440 | tf_op jit(solution)/shard_map/all_gather | solution.py:63
  10.1 20.6 %collective-permute-start = (bf16[385,1024]{1,0:T(8,128)(2,1)S(1)}, bf16[385,1024]{1,0:T(8,128)(2,1)S(1)}, u32[]{:S(2)}, u32[]{:S(2)}) collective-permute-start(bf16[385,1024]{1,0:T(8,128)(2,1)S(1)} %constant_dynamic-update-slice_fusion), channel_id=1, source_target_pairs={{0,3},{1,0},{2,1},{3,2},{4,7},{5,4},{6,5},{7,6},{8,11},{9,8},{10,9... | collective-permute-start | bytes 2365448 | tf_op jit(solution)/shard_map/ppermute | solution.py:38
  12.5 36.3 %collective-permute-start.1 = (bf16[385,1024]{1,0:T(8,128)(2,1)S(1)}, bf16[385,1024]{1,0:T(8,128)(2,1)S(1)}, u32[]{:S(2)}, u32[]{:S(2)}) collective-permute-start(bf16[385,1024]{1,0:T(8,128)(2,1)S(1)} %constant_dynamic-update-slice_fusion), channel_id=1, source_target_pairs={{0,2},{1,3},{2,0},{3,1},{4,6},{5,7},{6,4},{7,5},{8,10},{9,11},{10,... | collective-permute-start | bytes 2365448 | tf_op jit(solution)/shard_map/ppermute | solution.py:38
  13.2 35.7 %collective-permute-start.2 = (bf16[385,1024]{1,0:T(8,128)(2,1)S(1)}, bf16[385,1024]{1,0:T(8,128)(2,1)S(1)}, u32[]{:S(2)}, u32[]{:S(2)}) collective-permute-start(bf16[385,1024]{1,0:T(8,128)(2,1)S(1)} %constant_dynamic-update-slice_fusion), channel_id=1, source_target_pairs={{0,1},{1,2},{2,3},{3,0},{4,5},{5,6},{6,7},{7,4},{8,9},{9,10},{10,1... | collective-permute-start | bytes 2365448 | tf_op jit(solution)/shard_map/ppermute | solution.py:38
  13.4 4.3 %copy-start.15 = (f32[32,64]{1,0:T(8,128)S(1)}, f32[32,64]{1,0:T(8,128)}, u32[]{:S(2)}) copy-start(f32[32,64]{1,0:T(8,128)} %param.14) | copy-start | bytes 24580
  13.4 4.3 %copy-start.16 = (f32[32,64]{1,0:T(8,128)S(1)}, f32[32,64]{1,0:T(8,128)}, u32[]{:S(2)}) copy-start(f32[32,64]{1,0:T(8,128)} %param.13) | copy-start | bytes 24580
  13.4 6.2 %copy-start.14 = (f32[3,3,512]{2,1,0:T(4,128)S(1)}, f32[3,3,512]{2,1,0:T(4,128)}, u32[]{:S(2)}) copy-start(f32[3,3,512]{2,1,0:T(4,128)} %param.12) | copy-start | bytes 55300
  13.4 254.2 %all-gather.9.cloned.1.call-start = ((), (), s32[]{:S(2)}) async-start(), calls=%async_computation | async-start | bytes 1966080 | tf_op jit(solution)/shard_map/all_gather | solution.py:138
  17.7 2.5 copy-start.10
  71.7 85.5 %collective-permute-start.3 = (bf16[3,512,512]{2,1,0:T(8,128)(2,1)}, bf16[3,512,512]{2,1,0:T(8,128)(2,1)}, u32[]{:S(2)}, u32[]{:S(2)}) collective-permute-start(bf16[3,512,512]{2,1,0:T(8,128)(2,1)} %fusion.9), channel_id=1, source_target_pairs={{0,16},{16,0},{1,17},{17,1},{2,18},{18,2},{3,19},{19,3},{4,20},{20... | collective-permute-start | bytes 4718600 | tf_op jit(solution)/shard_map/ppermute | solution.py:69
  103.8 4.7 %copy-start.1 = (bf16[384,4,1,512]{3,2,1,0:T(2,128)(2,1)S(1)}, bf16[384,4,1,512]{3,2,1,0:T(2,128)(2,1)}, u32[]{:S(2)}) copy-start(bf16[384,4,1,512]{3,2,1,0:T(2,128)(2,1)} %get-tuple-element.89) | copy-start | bytes 4718596
  107.1 52.4 %collective-permute-start.4 = (bf16[3,512,512]{2,1,0:T(8,128)(2,1)}, bf16[3,512,512]{2,1,0:T(8,128)(2,1)}, u32[]{:S(2)}, u32[]{:S(2)}) collective-permute-start(bf16[3,512,512]{2,1,0:T(8,128)(2,1)} %fusion.8), channel_id=1, source_target_pairs={{0,16},{16,0},{1,17},{17,1},{2,18},{18,2},{3,19},{19,3},{4,20},{20... | collective-permute-start | bytes 4718600 | tf_op jit(solution)/shard_map/ppermute | solution.py:69
  108.5 3.7 %copy-start.6 = (bf16[2048,1,512]{2,0,1:T(8,128)(2,1)S(1)}, bf16[2048,1,512]{2,0,1:T(8,128)(2,1)}, u32[]{:S(2)}) copy-start(bf16[2048,1,512]{2,0,1:T(8,128)(2,1)} %all-gather.13.cloned.1.call-done) | copy-start | bytes 6291460
  113.3 40.4 %copy-start.5 = (bf16[1024,1,512]{2,0,1:T(8,128)(2,1)S(1)}, bf16[1024,1,512]{2,0,1:T(8,128)(2,1)}, u32[]{:S(2)}) copy-start(bf16[1024,1,512]{2,0,1:T(8,128)(2,1)} %get-tuple-element.82) | copy-start | bytes 3145732
  149.9 3.9 %copy-start.9 = (f32[384,512]{1,0:T(8,128)S(1)}, f32[384,512]{1,0:T(8,128)}, u32[]{:S(2)}) copy-start(f32[384,512]{1,0:T(8,128)} %convolution_bitcast_fusion.5) | copy-start | bytes 2359300
  149.9 4.3 %copy-start.4 = (bf16[1024,1,512]{2,0,1:T(8,128)(2,1)S(1)}, bf16[1024,1,512]{2,0,1:T(8,128)(2,1)}, u32[]{:S(2)}) copy-start(bf16[1024,1,512]{2,0,1:T(8,128)(2,1)} %get-tuple-element.84) | copy-start | bytes 3145732
  149.9 4.7 %copy-start.7 = (bf16[2048,1,512]{2,0,1:T(8,128)(2,1)S(1)}, bf16[2048,1,512]{2,0,1:T(8,128)(2,1)}, u32[]{:S(2)}) copy-start(bf16[2048,1,512]{2,0,1:T(8,128)(2,1)} %all-gather.15.cloned.1.call-done) | copy-start | bytes 6291460
  152.2 36.0 %collective-permute-start.5 = (bf16[3,512,512]{2,1,0:T(8,128)(2,1)S(1)}, bf16[3,512,512]{2,1,0:T(8,128)(2,1)S(1)}, u32[]{:S(2)}, u32[]{:S(2)}) collective-permute-start(bf16[3,512,512]{2,1,0:T(8,128)(2,1)S(1)} %fusion.7), channel_id=1, source_target_pairs={{0,16},{16,0},{1,17},{17,1},{2,18},{18,2},{3,19},{19,3},{4,20},{20... | collective-permute-start | bytes 4718600 | tf_op jit(solution)/shard_map/ppermute | solution.py:69
  153.7 1.9 copy-start.2
  155.6 1.2 copy-start.3
  161.6 29.6 %copy-start.13 = (f32[1,3,512]{2,1,0:T(4,128)S(1)}, f32[1,3,512]{2,1,0:T(4,128)}, u32[]{:S(2)}) copy-start(f32[1,3,512]{2,1,0:T(4,128)} %get-tuple-element.90) | copy-start | bytes 18436
  161.6 29.6 %copy-start.12 = (f32[1,3,512]{2,1,0:T(4,128)S(1)}, f32[1,3,512]{2,1,0:T(4,128)}, u32[]{:S(2)}) copy-start(f32[1,3,512]{2,1,0:T(4,128)} %get-tuple-element.92) | copy-start | bytes 18436
  161.6 29.7 %copy-start.11 = (f32[1,3,512]{2,1,0:T(4,128)S(1)}, f32[1,3,512]{2,1,0:T(4,128)}, u32[]{:S(2)}) copy-start(f32[1,3,512]{2,1,0:T(4,128)} %get-tuple-element.91) | copy-start | bytes 18436
  161.7 29.7 %copy-start.17 = (f32[32,1,128]{2,1,0:T(1,128)S(1)}, f32[32,1,128]{2,1,0:T(1,128)}, u32[]{:S(2)}) copy-start(f32[32,1,128]{2,1,0:T(1,128)} %fusion.26) | copy-start | bytes 49156
  189.0 16.9 %collective-permute-start.6 = (bf16[2,1536]{1,0:T(2,128)(2,1)S(1)}, bf16[2,1536]{1,0:T(2,128)(2,1)S(1)}, u32[]{:S(2)}, u32[]{:S(2)}) collective-permute-start(bf16[2,1536]{1,0:T(2,128)(2,1)S(1)} %pad_maximum_fusion.1), channel_id=1, source_target_pairs={{0,4},{4,8},{8,12},{1,5},{5,9},{9,13},{2,6},{6,10},{10,14},{3,7},{... | collective-permute-start | bytes 18440 | tf_op jit(solution)/shard_map/ppermute | solution.py:12
  216.3 23.9 %copy-start = (f32[32,128,255]{2,1,0:T(8,128)S(1)}, f32[32,128,255]{2,1,0:T(8,128)}, u32[]{:S(2)}) copy-start(f32[32,128,255]{2,1,0:T(8,128)} %reshape.86) | copy-start | bytes 12533764
Sparse Core Ops, SparseCore 0:
  9.3 48.3 all-gather.10
  59.3 44.4 all-gather.12
  105.4 44.4 all-gather.14
  248.7 18.9 all-gather.8

commit v2 on v1

--- a/solution.py
+++ b/solution.py
@@ -57,10 +57,23 @@
     piece = shard_rows // n_grp
     streams = w_in.shape[1]
 
+    span = short_taps.shape[0]
+    halo = span - 1
+    decay = rates[:, :, None]
+    coef = residues * jnp.sqrt(-jnp.expm1(-2.0 * rates)) * mode_count ** (-0.5)
+    lags = jnp.arange(block_rows).astype(jnp.float32)
+    powers = jnp.exp(-decay * lags)
+    long_taps = jnp.einsum("gn,gnt->gt", coef, powers, precision=highest)
+    kernel = banded(long_taps[:, ::-1])[:, :, reach:]
+    tail = jnp.exp(-decay * (reach - lags))
+    entry = coef[:, None, :] * jnp.exp(-rates[:, None, :] * (lags[None, :, None] + 1.0))
+
     own = lax.dynamic_slice_in_dim(w_in, me_grp * piece, piece, axis=0)
     relayed = []
     for s in range(streams):
         got = lax.all_gather(own[:, s, :], "ctx", axis=0)
+        if s == 0:
+            got, kernel, tail, entry = lax.optimization_barrier((got, kernel, tail, entry))
         doubled = jnp.concatenate([got, got], axis=0)
         send = lax.dynamic_slice_in_dim(doubled, me_ctx + 1, n_ctx - 1, axis=0)
         received = []
@@ -69,14 +82,16 @@
             received.append(lax.ppermute(send, "grp", pairs))
         relayed.append((got, received))
 
-    with_gain = jnp.concatenate([tokens, norm_gain[None]], axis=0)
+    before = shifted(tokens[tok_rows - halo :], "ctx", 1)
+    with_gain = jnp.concatenate([before, tokens, norm_gain[None]], axis=0)
     stacked = gather_by_permutes(with_gain, "tp")
     gathered = jnp.concatenate(list(stacked), axis=1)
-    values = gathered[:tok_rows].astype(jnp.float32)
-    gain_whole = gathered[tok_rows]
+    ext_rows = tok_rows + halo
+    values = gathered[:ext_rows].astype(jnp.float32)
+    gain_whole = gathered[ext_rows]
     scale = lax.rsqrt(jnp.mean(values * values, axis=1, keepdims=True) + 1e-06)
     normed = (values * scale * gain_whole.astype(jnp.float32)).astype(jnp.bfloat16)
-    normed4 = normed.reshape(tok_rows, n_ctx, n_grp, piece)
+    normed4 = normed.reshape(ext_rows, n_ctx, n_grp, piece)
     mine = lax.dynamic_index_in_dim(normed4, me_grp, axis=2, keepdims=False)
     others = []
     for by in range(1, n_grp):
@@ -94,23 +109,14 @@
                 "tkr,krc->tc", part[:, 1:], recv, preferred_element_type=jnp.float32
             )
         outputs.append(acc)
-    projected = jnp.concatenate(outputs, axis=1).astype(jnp.bfloat16)
-    span = short_taps.shape[0]
+    extended = jnp.concatenate(outputs, axis=1).astype(jnp.bfloat16)
     taps = short_taps.reshape(span, 3 * local_width)
-    before = shifted(projected[tok_rows - (span - 1) :], "ctx", 1)
-    filtered = short_filter(jnp.concatenate([before, projected], axis=0), taps, tok_rows)
+    filtered = short_filter(extended, taps, tok_rows)
     product = filtered[:, :local_width] * filtered[:, 2 * local_width :]
     second = filtered[:, local_width : 2 * local_width]
-    decay = rates[:, :, None]
-    coef = residues * jnp.sqrt(-jnp.expm1(-2.0 * rates)) * mode_count ** (-0.5)
-    lags = jnp.arange(block_rows).astype(jnp.float32)
-    powers = jnp.exp(-decay * lags)
-    long_taps = jnp.einsum("gn,gnt->gt", coef, powers, precision=highest)
-    kernel = banded(long_taps[:, ::-1])[:, :, reach:]
     blocks = tok_rows // block_rows
     current = product.reshape(blocks, block_rows, local_groups, group_size)
     near = jnp.einsum("gij,bjgc->bigc", kernel, current, precision=highest)
-    tail = jnp.exp(-decay * (reach - lags))
     ends = jnp.einsum("gni,bigc->bgnc", tail, current, precision=highest)
     step_decay = jnp.exp(-decay * block_rows)
 
@@ -119,18 +125,14 @@
 
     zero_state = jnp.zeros((local_groups, mode_count, group_size), jnp.float32)
     own_state, local_starts = lax.scan(advance, zero_state, ends)
-    position = lax.axis_index("ctx")
-    shards = lax.all_gather(own_state[None], "ctx", axis=0, tiled=True)
-    source = jnp.arange(shards.shape[0])
-    distance = (position - 1 - source).astype(jnp.float32)[:, None, None]
-    weight = jnp.where(
-        distance >= 0.0, jnp.exp(-rates[None] * tok_rows * jnp.maximum(distance, 0.0)), 0.0
-    )
-    incoming = jnp.einsum("kgn,kgnc->gnc", weight, shards, precision=highest)
+    incoming = jnp.zeros_like(own_state)
+    for by in range(1, n_ctx):
+        pairs = [(k, k + by) for k in range(n_ctx - by)]
+        arrived = lax.ppermute(own_state, "ctx", pairs)
+        incoming = incoming + jnp.exp(-decay * (tok_rows * (by - 1.0))) * arrived
     block_index = jnp.arange(blocks).astype(jnp.float32)
     lead = jnp.exp(-decay[None] * block_rows * block_index[:, None, None, None])
     starts = lead * incoming[None] + local_starts
-    entry = coef[:, None, :] * jnp.exp(-rates[:, None, :] * (lags[None, :, None] + 1.0))
     distant = jnp.einsum("gin,bgnc->bigc", entry, starts, precision=highest)
     conv_out = (near + distant).reshape(tok_rows, local_width)
     gated = (second * conv_out).astype(jnp.bfloat16)

time: 280 us -> 274 us (0.979)
  blocking collectives: 21 us -> 0 us
  waiting for transfers between devices: 142 us -> 124 us
  local copies, waits for them, and re-layouts: 41.9 us -> 55.1 us
  starting transfers between devices: 9.7 us -> 19.9 us
  other arithmetic: 21.6 us -> 27.2 us
    ppermute x3, waiting for transfers between devices: 28.6 us -> 5.74 us  [gather_by_permutes(): pieces.append(lax.ppermute(x, axis, pairs))]
    all_gather x1 -> x0, blocking collectives: 21 us -> none  [body(): shards = lax.all_gather(own_state[None], 'ctx', axis=0, tiled=True)]
    all_gather x3, waiting for transfers between devices: 66.9 us -> 52.6 us  [body(): got = lax.all_gather(own[:, s, :], 'ctx', axis=0)]
    ppermute x0 -> x3, waiting for transfers between devices: none -> 10.9 us  [body(): arrived = lax.ppermute(own_state, 'ctx', pairs)]
    all_gather x1, waiting for transfers between devices: 19.1 us -> 27.7 us  [body(): lax.all_gather(gated, 'tp', axis=1, tiled=True)]
    ppermute x0 -> x3, starting transfers between devices: none -> 8.06 us  [body(): arrived = lax.ppermute(own_state, 'ctx', pairs)]
    slice x0 -> x2, local copies, waits for them, and re-layouts: none -> 4.17 us  [the longest x1 4.17 us: body(): kernel = banded(long_taps[:, ::-1])[:, :, reach:]]
    ppermute x1, starting transfers between devices: 1.69 us -> 4.96 us  [shifted(): return lax.ppermute(x, axis, pairs)]
  transfers between devices with their start and end apart: 11 -> 14, of which waited for: 6 -> 9; matrix products, arithmetic and copies ran while one was open for 22% -> 30% of each run, Pallas kernels for 0% -> 0%
where the time goes in v2:
time: 274 us; the launch traced here: 271 us
  waiting for transfers between devices  124 us (45%)
  local copies, waits for them, and re-layouts  55.1 us (20%)
  matrix products  30.9 us (11%)
  other arithmetic  27.2 us (10%)
  starting transfers between devices  19.9 us (7%)
  between operations  13.9 us (5%)
    all_gather x3, waiting for transfers between devices, body(): got = lax.all_gather(own[:, s, :], 'ctx', axis=0)  52.6 us
    all_gather x1, waiting for transfers between devices, body(): lax.all_gather(gated, 'tp', axis=1, tiled=True)  27.7 us
    ppermute x3, waiting for transfers between devices, body(): received.append(lax.ppermute(send, 'grp', pairs))  26.3 us
    ppermute x3, waiting for transfers between devices, body(): arrived = lax.ppermute(own_state, 'ctx', pairs)  10.9 us
    reshape x1, local copies, waits for them, and re-layouts, banded(): tiled[:, :length * (2 * length - 1)]  9.4 us
    concatenate x3, other arithmetic, body(): doubled = jnp.concatenate([got, got], axis=0)  8.74 us
    dynamic_slice x1, local copies, waits for them, and re-layouts, body(): part = lax.dynamic_index_in_dim(normed4, src_grp, axis=2, keepdims=False)  8.16 us
    ppermute x3, starting transfers between devices, body(): arrived = lax.ppermute(own_state, 'ctx', pairs)  8.06 us
  transfers between devices with their start and end apart: 14, of which 9 were waited for; matrix products, arithmetic and copies ran while one was open for 30% of the time, Pallas kernels for 0%

profile of v2, /device:TPU:0, one launch (start us, length us, event | category | flops | bytes accessed | tf_op | source)
XLA Modules:
  0.0 270.9 jit_solution(12692687402069742857)
XLA Ops:
  6.5 2.7 constant_dynamic-slice_fusion.1
  10.1 5.0 %collective-permute-start = (bf16[2,1024]{1,0:T(2,128)(2,1)S(1)}, bf16[2,1024]{1,0:T(2,128)(2,1)S(1)}, u32[]{:S(2)}, u32[]{:S(2)}) collective-permute-start(bf16[2,1024]{1,0:T(2,128)(2,1)S(1)} %slice.74), channel_id=1, source_target_pairs={{0,4},{4,8},{8,12},{1,5},{5,9},{9,13},{2,6},{6,10},{10,14},{3,7},{... | collective-permute-start | bytes 12296 | tf_op jit(solution)/shard_map/ppermute | solution.py:12
  15.2 3.7 %fusion.44 = (bf16[1024,1,512]{2,0,1:T(8,128)(2,1)}, bf16[1024,1,512]{2,0,1:T(8,128)(2,1)}, bf16[1024,1,512]{2,0,1:T(8,128)(2,1)}) fusion(bf16[1024,3,512]{2,0,1:T(8,128)(2,1)} %param.11), kind=kLoop, calls=%fused_computation.109 | loop fusion | bytes 6291456 | tf_op jit(solution)/shard_map/slice | solution.py:106
  29.9 2.4 copy.32
  32.4 2.2 slice.96
  34.6 9.4 %reshape.80 = f32[32,128,255]{2,1,0:T(8,128)} reshape(f32[32,32640]{1,0:T(8,128)} %slice.96) | data formatting | bytes 8355840 | tf_op jit(solution)/shard_map/reshape | solution.py:29
  44.0 4.2 %slice.97 = f32[32,128,128]{2,1,0:T(8,128)} slice(f32[32,128,255]{2,1,0:T(8,128)} %reshape.80), slice={[0:32], [0:128], [127:255]} | slice | bytes 4194304 | tf_op jit(solution)/shard_map/slice | solution.py:67
  51.4 2.3 exponential_multiply_fusion
  53.8 4.0 %collective-permute-done.2 = bf16[387,1024]{1,0:T(8,128)(2,1)S(1)} collective-permute-done((bf16[387,1024]{1,0:T(8,128)(2,1)}, bf16[387,1024]{1,0:T(8,128)(2,1)S(1)}, u32[]{:S(2)}, u32[]{:S(2)}) %collective-permute-start.2) | collective-permute-done | bytes 792608 | tf_op jit(solution)/shard_map/ppermute | solution.py:38
  62.4 2.8 %fusion.2 = bf16[386,4096]{1,0:T(8,128)(2,1)} fusion(f32[4096]{0:T(1024)S(1)} %bitcast.148, f32[386]{0:T(512)S(1)} %add_rsqrt_fusion, bf16[387,4096]{1,0:T(8,128)(2,1)S(1)} %pad_maximum_fusion), kind=kLoop, calls=%fused_computation.6 | loop fusion | flops 6324224 | bytes 6342152 | tf_op jit(solution)/shard_map/convert_element_type | solution.py:93
  65.1 7.4 %reshape.79 = bf16[386,4,2,512]{3,2,1,0:T(2,128)(2,1)S(1)} reshape(bf16[386,4096]{1,0:T(8,128)(2,1)} %fusion.2) | data formatting | bytes 6324224 | tf_op jit(solution)/shard_map/reshape | solution.py:94
  72.5 8.2 %constant_dynamic-slice_fusion.2 = (bf16[386,4,1,512]{3,2,1,0:T(2,128)(2,1)S(1)}, bf16[386,4,1,512]{3,2,1,0:T(2,128)(2,1)}) fusion(bf16[386,4,2,512]{3,2,1,0:T(2,128)(2,1)S(1)} %reshape.79, s32[]{:T(128)S(6)} %select_n.54, s32[]{:T(128)S(6)} %select_n.51), kind=kLoop, calls=%fused_computation.101 | loop fusion | bytes 6324232 | tf_op jit(solution)/shard_map/jit(dynamic_index_in_dim)/dynamic_slice | solution.py:99
  82.2 3.1 %fusion.10 = bf16[3,512,512]{2,1,0:T(8,128)(2,1)} fusion(s32[]{:T(128)S(6)} %select_n.58, bf16[4,512,512]{2,1,0:T(8,128)(2,1)} %bitcast.141), kind=kLoop, calls=%fused_computation.28 | loop fusion | flops 786432 | bytes 3670020 | tf_op jit(solution)/shard_map/concatenate | solution.py:77
  86.8 17.0 %all-gather.12.cloned.1.call-done = bf16[2048,1,512]{2,0,1:T(8,128)(2,1)} async-done(((bf16[512,1,512]{2,0,1:T(8,128)(2,1)}), bf16[2048,1,512]{2,0,1:T(8,128)(2,1)}) %all-gather.12.cloned.1.call-update) | async-done | bytes 2097168 | tf_op jit(solution)/shard_map/all_gather | solution.py:74
  103.8 3.3 %fusion.9 = bf16[3,512,512]{2,1,0:T(8,128)(2,1)} fusion(s32[]{:T(128)S(6)} %select_n.58, bf16[4,512,512]{2,1,0:T(8,128)(2,1)} %bitcast.145), kind=kLoop, calls=%fused_computation.27 | loop fusion | flops 786432 | bytes 3670020 | tf_op jit(solution)/shard_map/concatenate | solution.py:77
  108.6 3.8 %convolution_bitcast_fusion.5 = f32[386,512]{1,0:T(8,128)} fusion(bf16[4,512,512]{2,1,0:T(8,128)(2,1)} %bitcast.142, bf16[386,4,1,512]{3,2,1,0:T(2,128)(2,1)S(1)} %copy-done.4), kind=kOutput, calls=%fused_computation.35 | convolution fusion | flops 809500672 | bytes 4468736 | tf_op jit(solution)/shard_map/tkr,krc->tc/dot_general | solution.py:104
  114.4 35.5 %all-gather.14.cloned.1.call-done = bf16[2048,1,512]{2,0,1:T(8,128)(2,1)} async-done(((bf16[512,1,512]{2,0,1:T(8,128)(2,1)}), bf16[2048,1,512]{2,0,1:T(8,128)(2,1)}) %all-gather.14.cloned.1.call-update) | async-done | bytes 2097168 | tf_op jit(solution)/shard_map/all_gather | solution.py:74
  149.9 2.3 fusion.8
  157.5 2.2 fusion.22
  159.7 2.2 fusion.21
  161.9 26.3 %collective-permute-done.6 = bf16[3,512,512]{2,1,0:T(8,128)(2,1)S(1)} collective-permute-done((bf16[3,512,512]{2,1,0:T(8,128)(2,1)S(1)}, bf16[3,512,512]{2,1,0:T(8,128)(2,1)S(1)}, u32[]{:S(2)}, u32[]{:S(2)}) %collective-permute-start.6) | collective-permute-done | bytes 1572896 | tf_op jit(solution)/shard_map/ppermute | solution.py:82
  194.2 3.3 %convolution_bitcast_fusion.6 = f32[3,32,64,16]{2,3,0,1:T(8,128)S(1)} fusion(f32[32,64,128]{2,1,0:T(8,128)} %multiply_exponential_fusion, f32[3,128,32,16]{1,0,3,2:T(4,128)} %reshape.81), kind=kOutput, calls=%fused_computation.41 | convolution fusion | flops 150994944 | bytes 2228224 | tf_op jit(solution)/shard_map/gni,bigc->bgnc/dot_general | solution.py:120
  197.5 2.6 while.13
  200.1 3.5 %collective-permute-start.7 = (f32[32,64,16]{1,2,0:T(8,128)S(1)}, f32[32,64,16]{1,2,0:T(8,128)S(1)}, u32[]{:S(2)}, u32[]{:S(2)}) collective-permute-start(f32[32,64,16]{1,2,0:T(8,128)S(1)} %get-tuple-element.40), channel_id=1, source_target_pairs={{0,4},{4,8},{8,12},{1,5},{5,9},{9,13},{2,6},{6,10},{10,14},{3,7},{... | collective-permute-start | bytes 393224 | tf_op jit(solution)/shard_map/ppermute | solution.py:131
  203.7 3.0 %collective-permute-start.8 = (f32[32,64,16]{1,2,0:T(8,128)S(1)}, f32[32,64,16]{1,2,0:T(8,128)S(1)}, u32[]{:S(2)}, u32[]{:S(2)}) collective-permute-start(f32[32,64,16]{1,2,0:T(8,128)S(1)} %get-tuple-element.40), channel_id=1, source_target_pairs={{0,8},{4,12},{1,9},{5,13},{2,10},{6,14},{3,11},{7,15},{16,24},{20,... | collective-permute-start | bytes 393224 | tf_op jit(solution)/shard_map/ppermute | solution.py:131
  210.2 5.7 %collective-permute-done.8 = f32[32,64,16]{1,2,0:T(8,128)S(1)} collective-permute-done((f32[32,64,16]{1,2,0:T(8,128)S(1)}, f32[32,64,16]{1,2,0:T(8,128)S(1)}, u32[]{:S(2)}, u32[]{:S(2)}) %collective-permute-start.8) | collective-permute-done | bytes 131104 | tf_op jit(solution)/shard_map/ppermute | solution.py:131
  215.8 3.3 %collective-permute-done.9 = f32[32,64,16]{1,2,0:T(8,128)S(1)} collective-permute-done((f32[32,64,16]{1,2,0:T(8,128)S(1)}, f32[32,64,16]{1,2,0:T(8,128)S(1)}, u32[]{:S(2)}, u32[]{:S(2)}) %collective-permute-start.9) | collective-permute-done | bytes 131104 | tf_op jit(solution)/shard_map/ppermute | solution.py:131
  219.3 2.6 fusion.23
  221.9 3.4 %fusion.14 = f32[3,128,32,16]{1,3,0,2:T(8,128)S(1)} fusion(f32[32,3,16,128]{3,2,1,0:T(8,128)S(1)} %fusion.23, f32[32,128,128]{2,1,0:T(8,128)S(1)} %copy-done, f32[3,128,32,16]{1,0,3,2:T(4,128)S(1)} %copy-done.3), kind=kOutput, calls=%fused_computation.40 | convolution fusion | flops 302186496 | bytes 4456448 | tf_op jit(solution)/shard_map/gij,bjgc->bigc/dot_general | solution.py:119
  226.7 2.4 copy.23
  231.1 27.7 %all-gather.8.cloned.1.call-done = bf16[384,2048]{1,0:T(8,128)(2,1)} async-done(((bf16[384,512]{1,0:T(8,128)(2,1)}), bf16[384,2048]{1,0:T(8,128)(2,1)}) %all-gather.8.cloned.1.call-update) | async-done | bytes 1572880 | tf_op jit(solution)/shard_map/all_gather | solution.py:140
  258.8 5.3 %add_convert_fusion = bf16[384,1024]{1,0:T(8,128)(2,1)} fusion(bf16[384,1024]{1,0:T(8,128)(2,1)S(1)} %copy-done.2, bf16[384,2048]{1,0:T(8,128)(2,1)} %all-gather.8.cloned.1.call-done, bf16[2048,1024]{1,0:T(8,128)(2,1)} %param.15), kind=kOutput, calls=%fused_computation.29 | convolution fusion | flops 1611792384 | bytes 7340032 | tf_op jit(solution)/shard_map/dot_general | solution.py:139
  (122 shorter events, 46.9 us)
Async XLA Ops:
  6.5 3.5 %copy-start.1 = (bf16[384,1024]{1,0:T(8,128)(2,1)S(1)}, bf16[384,1024]{1,0:T(8,128)(2,1)}, u32[]{:S(2)}) copy-start(bf16[384,1024]{1,0:T(8,128)(2,1)} %param.9) | copy-start | bytes 2359300
  6.5 75.6 %all-gather.10.cloned.1.call-start = ((), (), s32[]{:S(2)}) async-start(), calls=%async_computation.1 | async-start | bytes 2621440 | tf_op jit(solution)/shard_map/all_gather | solution.py:74
  9.2 94.6 %all-gather.12.cloned.1.call-start = ((), (), s32[]{:S(2)}) async-start(), calls=%async_computation.2 | async-start | bytes 2621440 | tf_op jit(solution)/shard_map/all_gather | solution.py:74
  10.0 139.9 %all-gather.14.cloned.1.call-start = ((), (), s32[]{:S(2)}) async-start(), calls=%async_computation.3 | async-start | bytes 2621440 | tf_op jit(solution)/shard_map/all_gather | solution.py:74
  10.1 10.7 %collective-permute-start = (bf16[2,1024]{1,0:T(2,128)(2,1)S(1)}, bf16[2,1024]{1,0:T(2,128)(2,1)S(1)}, u32[]{:S(2)}, u32[]{:S(2)}) collective-permute-start(bf16[2,1024]{1,0:T(2,128)(2,1)S(1)} %slice.74), channel_id=1, source_target_pairs={{0,4},{4,8},{8,12},{1,5},{5,9},{9,13},{2,6},{6,10},{10,14},{3,7},{... | collective-permute-start | bytes 12296 | tf_op jit(solution)/shard_map/ppermute | solution.py:12
  15.1 243.7 %all-gather.8.cloned.1.call-start = ((), (), s32[]{:S(2)}) async-start(), calls=%async_computation | async-start | bytes 1966080 | tf_op jit(solution)/shard_map/all_gather | solution.py:140
  15.1 3.7 %copy-start.18 = (f32[32,64]{1,0:T(8,128)S(1)}, f32[32,64]{1,0:T(8,128)}, u32[]{:S(2)}) copy-start(f32[32,64]{1,0:T(8,128)} %param.13) | copy-start | bytes 24580
  15.1 3.7 %copy-start.19 = (f32[32,64]{1,0:T(8,128)S(1)}, f32[32,64]{1,0:T(8,128)}, u32[]{:S(2)}) copy-start(f32[32,64]{1,0:T(8,128)} %param.14) | copy-start | bytes 24580
  15.1 5.6 %copy-start.20 = (bf16[1024]{0:T(1024)(128)(2,1)S(1)}, bf16[1024]{0:T(1024)(128)(2,1)}, u32[]{:S(2)}) copy-start(bf16[1024]{0:T(1024)(128)(2,1)} %param.10) | copy-start | bytes 6148
  18.9 6.3 %copy-start.17 = (f32[3,3,512]{2,1,0:T(4,128)S(1)}, f32[3,3,512]{2,1,0:T(4,128)}, u32[]{:S(2)}) copy-start(f32[3,3,512]{2,1,0:T(4,128)} %param.12) | copy-start | bytes 55300
  19.5 3.1 %copy-start.12 = (f32[32,64]{1,0:T(8,128)}, f32[32,64]{1,0:T(8,128)S(1)}, u32[]{:S(2)}) copy-start(f32[32,64]{1,0:T(8,128)S(1)} %get-tuple-element.102) | copy-start | bytes 24580
  21.9 31.8 %collective-permute-start.1 = (bf16[387,1024]{1,0:T(8,128)(2,1)}, bf16[387,1024]{1,0:T(8,128)(2,1)S(1)}, u32[]{:S(2)}, u32[]{:S(2)}) collective-permute-start(bf16[387,1024]{1,0:T(8,128)(2,1)} %pad_maximum_fusion.1), channel_id=1, source_target_pairs={{0,3},{1,0},{2,1},{3,2},{4,7},{5,4},{6,5},{7,6},{8,11},{9,8},{10,9... | collective-permute-start | bytes 2377736 | tf_op jit(solution)/shard_map/ppermute | solution.py:38
  24.3 33.5 %collective-permute-start.2 = (bf16[387,1024]{1,0:T(8,128)(2,1)}, bf16[387,1024]{1,0:T(8,128)(2,1)S(1)}, u32[]{:S(2)}, u32[]{:S(2)}) collective-permute-start(bf16[387,1024]{1,0:T(8,128)(2,1)} %pad_maximum_fusion.1), channel_id=1, source_target_pairs={{0,2},{1,3},{2,0},{3,1},{4,6},{5,7},{6,4},{7,5},{8,10},{9,11},{10,... | collective-permute-start | bytes 2377736 | tf_op jit(solution)/shard_map/ppermute | solution.py:38
  26.2 33.3 %collective-permute-start.3 = (bf16[387,1024]{1,0:T(8,128)(2,1)}, bf16[387,1024]{1,0:T(8,128)(2,1)S(1)}, u32[]{:S(2)}, u32[]{:S(2)}) collective-permute-start(bf16[387,1024]{1,0:T(8,128)(2,1)} %pad_maximum_fusion.1), channel_id=1, source_target_pairs={{0,1},{1,2},{2,3},{3,0},{4,5},{5,6},{6,7},{7,4},{8,9},{9,10},{10,1... | collective-permute-start | bytes 2377736 | tf_op jit(solution)/shard_map/ppermute | solution.py:38
  85.3 72.2 %collective-permute-start.4 = (bf16[3,512,512]{2,1,0:T(8,128)(2,1)}, bf16[3,512,512]{2,1,0:T(8,128)(2,1)}, u32[]{:S(2)}, u32[]{:S(2)}) collective-permute-start(bf16[3,512,512]{2,1,0:T(8,128)(2,1)} %fusion.10), channel_id=1, source_target_pairs={{0,16},{16,0},{1,17},{17,1},{2,18},{18,2},{3,19},{19,3},{4,20},{20... | collective-permute-start | bytes 4718600 | tf_op jit(solution)/shard_map/ppermute | solution.py:82
  103.8 4.8 %copy-start.4 = (bf16[386,4,1,512]{3,2,1,0:T(2,128)(2,1)S(1)}, bf16[386,4,1,512]{3,2,1,0:T(2,128)(2,1)}, u32[]{:S(2)}) copy-start(bf16[386,4,1,512]{3,2,1,0:T(2,128)(2,1)} %get-tuple-element.86) | copy-start | bytes 4743172
  107.1 52.6 %collective-permute-start.5 = (bf16[3,512,512]{2,1,0:T(8,128)(2,1)}, bf16[3,512,512]{2,1,0:T(8,128)(2,1)}, u32[]{:S(2)}, u32[]{:S(2)}) collective-permute-start(bf16[3,512,512]{2,1,0:T(8,128)(2,1)} %fusion.9), channel_id=1, source_target_pairs={{0,16},{16,0},{1,17},{17,1},{2,18},{18,2},{3,19},{19,3},{4,20},{20... | collective-permute-start | bytes 4718600 | tf_op jit(solution)/shard_map/ppermute | solution.py:82
  108.6 3.8 %copy-start.10 = (bf16[2048,1,512]{2,0,1:T(8,128)(2,1)S(1)}, bf16[2048,1,512]{2,0,1:T(8,128)(2,1)}, u32[]{:S(2)}) copy-start(bf16[2048,1,512]{2,0,1:T(8,128)(2,1)} %all-gather.12.cloned.1.call-done) | copy-start | bytes 6291460
  114.4 39.4 %copy-start.8 = (bf16[1024,1,512]{2,0,1:T(8,128)(2,1)S(1)}, bf16[1024,1,512]{2,0,1:T(8,128)(2,1)}, u32[]{:S(2)}) copy-start(bf16[1024,1,512]{2,0,1:T(8,128)(2,1)} %get-tuple-element.87) | copy-start | bytes 3145732
  149.9 5.5 %copy-start.7 = (bf16[1024,1,512]{2,0,1:T(8,128)(2,1)S(1)}, bf16[1024,1,512]{2,0,1:T(8,128)(2,1)}, u32[]{:S(2)}) copy-start(bf16[1024,1,512]{2,0,1:T(8,128)(2,1)} %get-tuple-element.89) | copy-start | bytes 3145732
  149.9 5.5 %copy-start.11 = (f32[386,512]{1,0:T(8,128)S(1)}, f32[386,512]{1,0:T(8,128)}, u32[]{:S(2)}) copy-start(f32[386,512]{1,0:T(8,128)} %convolution_bitcast_fusion.4) | copy-start | bytes 2371588
  149.9 5.9 %copy-start.9 = (bf16[2048,1,512]{2,0,1:T(8,128)(2,1)S(1)}, bf16[2048,1,512]{2,0,1:T(8,128)(2,1)}, u32[]{:S(2)}) copy-start(bf16[2048,1,512]{2,0,1:T(8,128)(2,1)} %all-gather.14.cloned.1.call-done) | copy-start | bytes 6291460
  152.2 36.0 %collective-permute-start.6 = (bf16[3,512,512]{2,1,0:T(8,128)(2,1)S(1)}, bf16[3,512,512]{2,1,0:T(8,128)(2,1)S(1)}, u32[]{:S(2)}, u32[]{:S(2)}) collective-permute-start(bf16[3,512,512]{2,1,0:T(8,128)(2,1)S(1)} %fusion.8), channel_id=1, source_target_pairs={{0,16},{16,0},{1,17},{17,1},{2,18},{18,2},{3,19},{19,3},{4,20},{20... | collective-permute-start | bytes 4718600 | tf_op jit(solution)/shard_map/ppermute | solution.py:82
  153.8 2.1 copy-start.5
  197.5 10.7 %copy-start.13 = (f32[32,64]{1,0:T(8,128)S(1)}, f32[32,64]{1,0:T(8,128)}, u32[]{:S(2)}) copy-start(f32[32,64]{1,0:T(8,128)} %get-tuple-element.96) | copy-start | bytes 24580
  197.5 10.7 %copy-start.21 = (f32[3]{0:T(128)S(1)}, f32[3]{0:T(128)}, u32[]{:S(2)}) copy-start(f32[3]{0:T(128)} %iota_convert_fusion) | copy-start | bytes 40
  200.1 21.8 %copy-start = (f32[32,128,128]{2,1,0:T(8,128)S(1)}, f32[32,128,128]{2,1,0:T(8,128)}, u32[]{:S(2)}) copy-start(f32[32,128,128]{2,1,0:T(8,128)} %slice.97) | copy-start | bytes 6291460
  200.1 21.8 %copy-start.3 = (f32[3,128,32,16]{1,0,3,2:T(4,128)S(1)}, f32[3,128,32,16]{1,0,3,2:T(4,128)}, u32[]{:S(2)}) copy-start(f32[3,128,32,16]{1,0,3,2:T(4,128)} %reshape.81) | copy-start | bytes 2359300
  200.1 10.1 %collective-permute-start.7 = (f32[32,64,16]{1,2,0:T(8,128)S(1)}, f32[32,64,16]{1,2,0:T(8,128)S(1)}, u32[]{:S(2)}, u32[]{:S(2)}) collective-permute-start(f32[32,64,16]{1,2,0:T(8,128)S(1)} %get-tuple-element.40), channel_id=1, source_target_pairs={{0,4},{4,8},{8,12},{1,5},{5,9},{9,13},{2,6},{6,10},{10,14},{3,7},{... | collective-permute-start | bytes 393224 | tf_op jit(solution)/shard_map/ppermute | solution.py:131
  203.7 12.2 %collective-permute-start.8 = (f32[32,64,16]{1,2,0:T(8,128)S(1)}, f32[32,64,16]{1,2,0:T(8,128)S(1)}, u32[]{:S(2)}, u32[]{:S(2)}) collective-permute-start(f32[32,64,16]{1,2,0:T(8,128)S(1)} %get-tuple-element.40), channel_id=1, source_target_pairs={{0,8},{4,12},{1,9},{5,13},{2,10},{6,14},{3,11},{7,15},{16,24},{20,... | collective-permute-start | bytes 393224 | tf_op jit(solution)/shard_map/ppermute | solution.py:131
  206.6 12.6 %collective-permute-start.9 = (f32[32,64,16]{1,2,0:T(8,128)S(1)}, f32[32,64,16]{1,2,0:T(8,128)S(1)}, u32[]{:S(2)}, u32[]{:S(2)}) collective-permute-start(f32[32,64,16]{1,2,0:T(8,128)S(1)} %get-tuple-element.40), channel_id=1, source_target_pairs={{0,12},{1,13},{2,14},{3,15},{16,28},{17,29},{18,30},{19,31}} | collective-permute-start | bytes 393224 | tf_op jit(solution)/shard_map/ppermute | solution.py:131
  226.7 32.1 %copy-start.2 = (bf16[384,1024]{1,0:T(8,128)(2,1)S(1)}, bf16[384,1024]{1,0:T(8,128)(2,1)}, u32[]{:S(2)}) copy-start(bf16[384,1024]{1,0:T(8,128)(2,1)} %param.9) | copy-start | bytes 2359300
  (4 other events, 3.3 us)
Sparse Core Ops, SparseCore 0:
  9.4 48.3 all-gather.9
  59.4 44.4 all-gather.11
  105.4 44.4 all-gather.13
  231.2 27.5 all-gather.7

commit v3 on v2

--- a/solution.py
+++ b/solution.py
@@ -69,10 +69,11 @@
     entry = coef[:, None, :] * jnp.exp(-rates[:, None, :] * (lags[None, :, None] + 1.0))
 
     own = lax.dynamic_slice_in_dim(w_in, me_grp * piece, piece, axis=0)
-    relayed = []
-    for s in range(streams):
+    order = [0, 2, 1] if streams == 3 else list(range(streams))
+    relayed = {}
+    for s in order:
         got = lax.all_gather(own[:, s, :], "ctx", axis=0)
-        if s == 0:
+        if s == order[0]:
             got, kernel, tail, entry = lax.optimization_barrier((got, kernel, tail, entry))
         doubled = jnp.concatenate([got, got], axis=0)
         send = lax.dynamic_slice_in_dim(doubled, me_ctx + 1, n_ctx - 1, axis=0)
@@ -80,7 +81,7 @@
         for by in range(1, n_grp):
             pairs = [(q, (q + by) % n_grp) for q in range(n_grp)]
             received.append(lax.ppermute(send, "grp", pairs))
-        relayed.append((got, received))
+        relayed[s] = (got, received)
 
     before = shifted(tokens[tok_rows - halo :], "ctx", 1)
     with_gain = jnp.concatenate([before, tokens, norm_gain[None]], axis=0)
@@ -98,8 +99,8 @@
         src_grp = (me_grp - by) % n_grp
         part = lax.dynamic_index_in_dim(normed4, src_grp, axis=2, keepdims=False)
         others.append((src_grp, jnp.roll(part, -me_ctx, axis=1)))
-    outputs = []
-    for s in range(streams):
+    filtered = {}
+    for s in order:
         got, received = relayed[s]
         acc = jnp.einsum("tkr,krc->tc", mine, got, preferred_element_type=jnp.float32)
         for (src_grp, part), recv in zip(others, received):
@@ -108,12 +109,9 @@
             acc = acc + jnp.einsum(
                 "tkr,krc->tc", part[:, 1:], recv, preferred_element_type=jnp.float32
             )
-        outputs.append(acc)
-    extended = jnp.concatenate(outputs, axis=1).astype(jnp.bfloat16)
-    taps = short_taps.reshape(span, 3 * local_width)
-    filtered = short_filter(extended, taps, tok_rows)
-    product = filtered[:, :local_width] * filtered[:, 2 * local_width :]
-    second = filtered[:, local_width : 2 * local_width]
+        filtered[s] = short_filter(acc.astype(jnp.bfloat16), short_taps[:, s, :], tok_rows)
+    product = filtered[0] * filtered[2]
+    second = filtered[1]
     blocks = tok_rows // block_rows
     current = product.reshape(blocks, block_rows, local_groups, group_size)
     near = jnp.einsum("gij,bjgc->bigc", kernel, current, precision=highest)

time: 274 us -> 265 us (0.967)
  local copies, waits for them, and re-layouts: 55.1 us -> 47.7 us
    mul x4 -> x1, local copies, waits for them, and re-layouts: 4.59 us -> 0.26 us  [body(): product = filtered[0] * filtered[2]]
    ppermute x3, waiting for transfers between devices: 5.74 us -> 9.36 us  [gather_by_permutes(): pieces.append(lax.ppermute(x, axis, pairs))]
    ppermute x3, waiting for transfers between devices: 10.9 us -> 8.01 us  [body(): arrived = lax.ppermute(own_state, 'ctx', pairs)]
  transfers between devices with their start and end apart: 14 -> 14, of which waited for: 9 -> 8; matrix products, arithmetic and copies ran while one was open for 30% -> 33% of each run, Pallas kernels for 0% -> 0%
where the time goes in v3:
time: 265 us; the launch traced here: 261 us
  waiting for transfers between devices  125 us (47%)
  local copies, waits for them, and re-layouts  47.7 us (18%)
  matrix products  29.9 us (11%)
  other arithmetic  24.8 us (9%)
  starting transfers between devices  19.9 us (8%)
  between operations  14 us (5%)
    all_gather x3, waiting for transfers between devices, body(): got = lax.all_gather(own[:, s, :], 'ctx', axis=0)  54 us
    all_gather x1, waiting for transfers between devices, body(): lax.all_gather(gated, 'tp', axis=1, tiled=True)  27.3 us
    ppermute x3, waiting for transfers between devices, body(): received.append(lax.ppermute(send, 'grp', pairs))  25.4 us
    reshape x1, local copies, waits for them, and re-layouts, banded(): tiled[:, :length * (2 * length - 1)]  9.4 us
    ppermute x3, waiting for transfers between devices, gather_by_permutes(): pieces.append(lax.ppermute(x, axis, pairs))  9.36 us
    concatenate x3, other arithmetic, body(): doubled = jnp.concatenate([got, got], axis=0)  9.17 us
    dynamic_slice x1, local copies, waits for them, and re-layouts, body(): part = lax.dynamic_index_in_dim(normed4, src_grp, axis=2, keepdims=False)  8.2 us
    ppermute x3, starting transfers between devices, body(): arrived = lax.ppermute(own_state, 'ctx', pairs)  8.09 us
  transfers between devices with their start and end apart: 14, of which 8 were waited for; matrix products, arithmetic and copies ran while one was open for 33% of the time, Pallas kernels for 0%

profile of v3, /device:TPU:0, one launch (start us, length us, event | category | flops | bytes accessed | tf_op | source)
XLA Modules:
  0.0 261.2 jit_solution(15785930868121278000)
XLA Ops:
  6.5 2.6 constant_dynamic-slice_fusion
  10.0 5.0 %collective-permute-start = (bf16[2,1024]{1,0:T(2,128)(2,1)S(1)}, bf16[2,1024]{1,0:T(2,128)(2,1)S(1)}, u32[]{:S(2)}, u32[]{:S(2)}) collective-permute-start(bf16[2,1024]{1,0:T(2,128)(2,1)S(1)} %slice.119), channel_id=1, source_target_pairs={{0,4},{4,8},{8,12},{1,5},{5,9},{9,13},{2,6},{6,10},{10,14},{3,7},{... | collective-permute-start | bytes 12296 | tf_op jit(solution)/shard_map/ppermute | solution.py:12
  15.0 3.6 %fusion.53 = (bf16[1024,1,512]{2,0,1:T(8,128)(2,1)}, bf16[1024,1,512]{2,0,1:T(8,128)(2,1)}, bf16[1024,1,512]{2,0,1:T(8,128)(2,1)}) fusion(bf16[1024,3,512]{2,0,1:T(8,128)(2,1)} %param.11), kind=kLoop, calls=%fused_computation.121 | loop fusion | bytes 6291456 | tf_op jit(solution)/shard_map/slice | solution.py:107
  29.5 2.4 copy.32
  31.9 2.2 slice.154
  34.1 9.4 %reshape.91 = f32[32,128,255]{2,1,0:T(8,128)} reshape(f32[32,32640]{1,0:T(8,128)} %slice.154) | data formatting | bytes 8355840 | tf_op jit(solution)/shard_map/reshape | solution.py:29
  43.6 4.2 %slice.155 = f32[32,128,128]{2,1,0:T(8,128)} slice(f32[32,128,255]{2,1,0:T(8,128)} %reshape.91), slice={[0:32], [0:128], [127:255]} | slice | bytes 4194304 | tf_op jit(solution)/shard_map/slice | solution.py:67
  47.7 2.3 exponential_multiply_fusion
  50.1 7.6 %collective-permute-done.2 = bf16[387,1024]{1,0:T(8,128)(2,1)S(1)} collective-permute-done((bf16[387,1024]{1,0:T(8,128)(2,1)}, bf16[387,1024]{1,0:T(8,128)(2,1)S(1)}, u32[]{:S(2)}, u32[]{:S(2)}) %collective-permute-start.2) | collective-permute-done | bytes 792608 | tf_op jit(solution)/shard_map/ppermute | solution.py:38
  57.7 1.8 collective-permute-done.3
  62.3 2.8 %fusion.2 = bf16[386,4096]{1,0:T(8,128)(2,1)} fusion(f32[4096]{0:T(1024)S(1)} %bitcast.163, f32[386]{0:T(512)S(1)} %add_rsqrt_fusion, bf16[387,4096]{1,0:T(8,128)(2,1)S(1)} %pad_maximum_fusion), kind=kLoop, calls=%fused_computation.6 | loop fusion | flops 6324224 | bytes 6342152 | tf_op jit(solution)/shard_map/convert_element_type | solution.py:94
  65.1 7.4 %reshape.90 = bf16[386,4,2,512]{3,2,1,0:T(2,128)(2,1)S(1)} reshape(bf16[386,4096]{1,0:T(8,128)(2,1)} %fusion.2) | data formatting | bytes 6324224 | tf_op jit(solution)/shard_map/reshape | solution.py:95
  72.5 8.2 %constant_dynamic-slice_fusion.2 = (bf16[386,4,1,512]{3,2,1,0:T(2,128)(2,1)S(1)}, bf16[386,4,1,512]{3,2,1,0:T(2,128)(2,1)}) fusion(bf16[386,4,2,512]{3,2,1,0:T(2,128)(2,1)S(1)} %reshape.90, s32[]{:T(128)S(6)} %select_n.54, s32[]{:T(128)S(6)} %select_n.51), kind=kLoop, calls=%fused_computation.113 | loop fusion | bytes 6324232 | tf_op jit(solution)/shard_map/jit(dynamic_index_in_dim)/dynamic_slice | solution.py:100
  82.2 3.7 %fusion.8 = bf16[3,512,512]{2,1,0:T(8,128)(2,1)} fusion(s32[]{:T(128)S(6)} %select_n.58, bf16[4,512,512]{2,1,0:T(8,128)(2,1)} %bitcast.158), kind=kLoop, calls=%fused_computation.23 | loop fusion | flops 786432 | bytes 3670020 | tf_op jit(solution)/shard_map/concatenate | solution.py:78
  87.4 16.3 %all-gather.12.cloned.1.call-done = bf16[2048,1,512]{2,0,1:T(8,128)(2,1)} async-done(((bf16[512,1,512]{2,0,1:T(8,128)(2,1)}), bf16[2048,1,512]{2,0,1:T(8,128)(2,1)}) %all-gather.12.cloned.1.call-update) | async-done | bytes 2097168 | tf_op jit(solution)/shard_map/all_gather | solution.py:75
  103.7 3.4 %fusion.7 = bf16[3,512,512]{2,1,0:T(8,128)(2,1)} fusion(s32[]{:T(128)S(6)} %select_n.58, bf16[4,512,512]{2,1,0:T(8,128)(2,1)} %bitcast.156), kind=kLoop, calls=%fused_computation.22 | loop fusion | flops 786432 | bytes 3670020 | tf_op jit(solution)/shard_map/concatenate | solution.py:78
  108.6 3.6 %convolution_bitcast_fusion.5 = f32[386,512]{1,0:T(8,128)} fusion(bf16[4,512,512]{2,1,0:T(8,128)(2,1)} %bitcast.159, bf16[386,4,1,512]{3,2,1,0:T(2,128)(2,1)S(1)} %copy-done.5), kind=kOutput, calls=%fused_computation.30 | convolution fusion | flops 809500672 | bytes 4468736 | tf_op jit(solution)/shard_map/tkr,krc->tc/dot_general | solution.py:105
  112.2 37.6 %all-gather.14.cloned.1.call-done = bf16[2048,1,512]{2,0,1:T(8,128)(2,1)} async-done(((bf16[512,1,512]{2,0,1:T(8,128)(2,1)}), bf16[2048,1,512]{2,0,1:T(8,128)(2,1)}) %all-gather.14.cloned.1.call-update) | async-done | bytes 2097168 | tf_op jit(solution)/shard_map/all_gather | solution.py:75
  149.8 2.1 fusion.6
  154.8 3.0 %convolution_bitcast_fusion.4 = f32[386,512]{1,0:T(8,128)S(1)} fusion(bf16[4,512,512]{2,1,0:T(8,128)(2,1)} %bitcast.157, bf16[386,4,1,512]{3,2,1,0:T(2,128)(2,1)S(1)} %copy-done.6), kind=kOutput, calls=%fused_computation.29 | convolution fusion | flops 809500672 | bytes 4468736 | tf_op jit(solution)/shard_map/tkr,krc->tc/dot_general | solution.py:105
  161.0 2.2 fusion.21
  163.2 25.4 %collective-permute-done.6 = bf16[3,512,512]{2,1,0:T(8,128)(2,1)S(1)} collective-permute-done((bf16[3,512,512]{2,1,0:T(8,128)(2,1)S(1)}, bf16[3,512,512]{2,1,0:T(8,128)(2,1)S(1)}, u32[]{:S(2)}, u32[]{:S(2)}) %collective-permute-start.6) | collective-permute-done | bytes 1572896 | tf_op jit(solution)/shard_map/ppermute | solution.py:83
  190.6 3.0 %convolution_bitcast_fusion.6 = f32[3,32,64,16]{2,3,0,1:T(8,128)S(1)} fusion(f32[32,64,128]{2,1,0:T(8,128)} %multiply_exponential_fusion, f32[3,128,32,16]{1,0,3,2:T(4,128)S(1)} %reshape.92), kind=kOutput, calls=%fused_computation.36 | convolution fusion | flops 150994944 | bytes 2228224 | tf_op jit(solution)/shard_map/gni,bigc->bgnc/dot_general | solution.py:118
  193.6 2.6 while.13
  196.2 3.6 %collective-permute-start.7 = (f32[32,64,16]{1,2,0:T(8,128)S(1)}, f32[32,64,16]{1,2,0:T(8,128)S(1)}, u32[]{:S(2)}, u32[]{:S(2)}) collective-permute-start(f32[32,64,16]{1,2,0:T(8,128)S(1)} %get-tuple-element.40), channel_id=1, source_target_pairs={{0,4},{4,8},{8,12},{1,5},{5,9},{9,13},{2,6},{6,10},{10,14},{3,7},{... | collective-permute-start | bytes 393224 | tf_op jit(solution)/shard_map/ppermute | solution.py:129
  199.8 2.9 %collective-permute-start.8 = (f32[32,64,16]{1,2,0:T(8,128)S(1)}, f32[32,64,16]{1,2,0:T(8,128)S(1)}, u32[]{:S(2)}, u32[]{:S(2)}) collective-permute-start(f32[32,64,16]{1,2,0:T(8,128)S(1)} %get-tuple-element.40), channel_id=1, source_target_pairs={{0,8},{4,12},{1,9},{5,13},{2,10},{6,14},{3,11},{7,15},{16,24},{20,... | collective-permute-start | bytes 393224 | tf_op jit(solution)/shard_map/ppermute | solution.py:129
  204.3 2.6 fusion.23
  206.9 4.3 %collective-permute-done.8 = f32[32,64,16]{1,2,0:T(8,128)S(1)} collective-permute-done((f32[32,64,16]{1,2,0:T(8,128)S(1)}, f32[32,64,16]{1,2,0:T(8,128)S(1)}, u32[]{:S(2)}, u32[]{:S(2)}) %collective-permute-start.8) | collective-permute-done | bytes 131104 | tf_op jit(solution)/shard_map/ppermute | solution.py:129
  211.3 3.7 %collective-permute-done.9 = f32[32,64,16]{1,2,0:T(8,128)S(1)} collective-permute-done((f32[32,64,16]{1,2,0:T(8,128)S(1)}, f32[32,64,16]{1,2,0:T(8,128)S(1)}, u32[]{:S(2)}, u32[]{:S(2)}) %collective-permute-start.9) | collective-permute-done | bytes 131104 | tf_op jit(solution)/shard_map/ppermute | solution.py:129
  216.3 3.4 %fusion.12 = f32[3,128,32,16]{1,3,0,2:T(8,128)S(1)} fusion(f32[32,3,16,128]{3,2,1,0:T(8,128)S(1)} %fusion.24, f32[32,128,128]{2,1,0:T(8,128)S(1)} %copy-done, f32[3,128,32,16]{1,0,3,2:T(4,128)S(1)} %reshape.92), kind=kOutput, calls=%fused_computation.35 | convolution fusion | flops 302186496 | bytes 4456448 | tf_op jit(solution)/shard_map/gij,bjgc->bigc/dot_general | solution.py:117
  221.8 27.3 %all-gather.8.cloned.1.call-done = bf16[384,2048]{1,0:T(8,128)(2,1)} async-done(((bf16[384,512]{1,0:T(8,128)(2,1)}), bf16[384,2048]{1,0:T(8,128)(2,1)}) %all-gather.8.cloned.1.call-update) | async-done | bytes 1572880 | tf_op jit(solution)/shard_map/all_gather | solution.py:138
  249.1 5.3 %add_convert_fusion = bf16[384,1024]{1,0:T(8,128)(2,1)} fusion(bf16[384,1024]{1,0:T(8,128)(2,1)S(1)} %copy-done.2, bf16[384,2048]{1,0:T(8,128)(2,1)} %all-gather.8.cloned.1.call-done, bf16[2048,1024]{1,0:T(8,128)(2,1)} %param.15), kind=kOutput, calls=%fused_computation.24 | convolution fusion | flops 1611792384 | bytes 7340032 | tf_op jit(solution)/shard_map/dot_general | solution.py:137
  (131 shorter events, 34.4 us)
Async XLA Ops:
  6.5 75.7 %all-gather.10.cloned.1.call-start = ((), (), s32[]{:S(2)}) async-start(), calls=%async_computation.1 | async-start | bytes 2621440 | tf_op jit(solution)/shard_map/all_gather | solution.py:75
  9.1 94.6 %all-gather.12.cloned.1.call-start = ((), (), s32[]{:S(2)}) async-start(), calls=%async_computation.2 | async-start | bytes 2621440 | tf_op jit(solution)/shard_map/all_gather | solution.py:75
  9.9 139.9 %all-gather.14.cloned.1.call-start = ((), (), s32[]{:S(2)}) async-start(), calls=%async_computation.3 | async-start | bytes 2621440 | tf_op jit(solution)/shard_map/all_gather | solution.py:75
  10.0 10.8 %collective-permute-start = (bf16[2,1024]{1,0:T(2,128)(2,1)S(1)}, bf16[2,1024]{1,0:T(2,128)(2,1)S(1)}, u32[]{:S(2)}, u32[]{:S(2)}) collective-permute-start(bf16[2,1024]{1,0:T(2,128)(2,1)S(1)} %slice.119), channel_id=1, source_target_pairs={{0,4},{4,8},{8,12},{1,5},{5,9},{9,13},{2,6},{6,10},{10,14},{3,7},{... | collective-permute-start | bytes 12296 | tf_op jit(solution)/shard_map/ppermute | solution.py:12
  15.0 5.7 %copy-start.28 = (bf16[1024]{0:T(1024)(128)(2,1)S(1)}, bf16[1024]{0:T(1024)(128)(2,1)}, u32[]{:S(2)}) copy-start(bf16[1024]{0:T(1024)(128)(2,1)} %param.10) | copy-start | bytes 6148
  15.0 234.1 %all-gather.8.cloned.1.call-start = ((), (), s32[]{:S(2)}) async-start(), calls=%async_computation | async-start | bytes 1966080 | tf_op jit(solution)/shard_map/all_gather | solution.py:138
  18.6 6.5 %copy-start.20 = (f32[3,3,512]{2,1,0:T(4,128)S(1)}, f32[3,3,512]{2,1,0:T(4,128)}, u32[]{:S(2)}) copy-start(f32[3,3,512]{2,1,0:T(4,128)} %param.12) | copy-start | bytes 55300
  21.9 28.2 %collective-permute-start.1 = (bf16[387,1024]{1,0:T(8,128)(2,1)}, bf16[387,1024]{1,0:T(8,128)(2,1)S(1)}, u32[]{:S(2)}, u32[]{:S(2)}) collective-permute-start(bf16[387,1024]{1,0:T(8,128)(2,1)} %pad_maximum_fusion.1), channel_id=1, source_target_pairs={{0,3},{1,0},{2,1},{3,2},{4,7},{5,4},{6,5},{7,6},{8,11},{9,8},{10,9... | collective-permute-start | bytes 2377736 | tf_op jit(solution)/shard_map/ppermute | solution.py:38
  24.2 33.5 %collective-permute-start.2 = (bf16[387,1024]{1,0:T(8,128)(2,1)}, bf16[387,1024]{1,0:T(8,128)(2,1)S(1)}, u32[]{:S(2)}, u32[]{:S(2)}) collective-permute-start(bf16[387,1024]{1,0:T(8,128)(2,1)} %pad_maximum_fusion.1), channel_id=1, source_target_pairs={{0,2},{1,3},{2,0},{3,1},{4,6},{5,7},{6,4},{7,5},{8,10},{9,11},{10,... | collective-permute-start | bytes 2377736 | tf_op jit(solution)/shard_map/ppermute | solution.py:38
  25.7 33.8 %collective-permute-start.3 = (bf16[387,1024]{1,0:T(8,128)(2,1)}, bf16[387,1024]{1,0:T(8,128)(2,1)S(1)}, u32[]{:S(2)}, u32[]{:S(2)}) collective-permute-start(bf16[387,1024]{1,0:T(8,128)(2,1)} %pad_maximum_fusion.1), channel_id=1, source_target_pairs={{0,1},{1,2},{2,3},{3,0},{4,5},{5,6},{6,7},{7,4},{8,9},{9,10},{10,1... | collective-permute-start | bytes 2377736 | tf_op jit(solution)/shard_map/ppermute | solution.py:38
  82.2 106.5 %copy-start.3 = (bf16[386,4,512]{2,0,1:T(8,128)(2,1)}, bf16[386,4,512]{2,0,1:T(8,128)(2,1)S(1)}, u32[]{:S(2)}) copy-start(bf16[386,4,512]{2,0,1:T(8,128)(2,1)S(1)} %fusion.5) | copy-start | bytes 4743172
  85.9 118.4 %collective-permute-start.4 = (bf16[3,512,512]{2,1,0:T(8,128)(2,1)}, bf16[3,512,512]{2,1,0:T(8,128)(2,1)}, u32[]{:S(2)}, u32[]{:S(2)}) collective-permute-start(bf16[3,512,512]{2,1,0:T(8,128)(2,1)} %fusion.8), channel_id=1, source_target_pairs={{0,16},{16,0},{1,17},{17,1},{2,18},{18,2},{3,19},{19,3},{4,20},{20... | collective-permute-start | bytes 4718600 | tf_op jit(solution)/shard_map/ppermute | solution.py:83
  107.1 53.9 %collective-permute-start.5 = (bf16[3,512,512]{2,1,0:T(8,128)(2,1)}, bf16[3,512,512]{2,1,0:T(8,128)(2,1)}, u32[]{:S(2)}, u32[]{:S(2)}) collective-permute-start(bf16[3,512,512]{2,1,0:T(8,128)(2,1)} %fusion.7), channel_id=1, source_target_pairs={{0,16},{16,0},{1,17},{17,1},{2,18},{18,2},{3,19},{19,3},{4,20},{20... | collective-permute-start | bytes 4718600 | tf_op jit(solution)/shard_map/ppermute | solution.py:83
  112.2 41.3 %copy-start.9 = (bf16[1024,1,512]{2,0,1:T(8,128)(2,1)S(1)}, bf16[1024,1,512]{2,0,1:T(8,128)(2,1)}, u32[]{:S(2)}) copy-start(bf16[1024,1,512]{2,0,1:T(8,128)(2,1)} %get-tuple-element.87) | copy-start | bytes 3145732
  151.9 36.7 %collective-permute-start.6 = (bf16[3,512,512]{2,1,0:T(8,128)(2,1)S(1)}, bf16[3,512,512]{2,1,0:T(8,128)(2,1)S(1)}, u32[]{:S(2)}, u32[]{:S(2)}) collective-permute-start(bf16[3,512,512]{2,1,0:T(8,128)(2,1)S(1)} %fusion.6), channel_id=1, source_target_pairs={{0,16},{16,0},{1,17},{17,1},{2,18},{18,2},{3,19},{19,3},{4,20},{20... | collective-permute-start | bytes 4718600 | tf_op jit(solution)/shard_map/ppermute | solution.py:83
  163.2 26.2 %copy-start.22 = (f32[1,1,512]{2,1,0:T(1,128)S(1)}, f32[1,1,512]{2,1,0:T(1,128)}, u32[]{:S(2)}) copy-start(f32[1,1,512]{2,1,0:T(1,128)} %get-tuple-element.94) | copy-start | bytes 6148
  163.2 26.2 %copy-start.23 = (f32[1,1,512]{2,1,0:T(1,128)S(1)}, f32[1,1,512]{2,1,0:T(1,128)}, u32[]{:S(2)}) copy-start(f32[1,1,512]{2,1,0:T(1,128)} %get-tuple-element.95) | copy-start | bytes 6148
  163.2 26.2 %copy-start.24 = (f32[1,1,512]{2,1,0:T(1,128)S(1)}, f32[1,1,512]{2,1,0:T(1,128)}, u32[]{:S(2)}) copy-start(f32[1,1,512]{2,1,0:T(1,128)} %get-tuple-element.96) | copy-start | bytes 6148
  163.2 26.2 %copy-start.25 = (f32[1,1,512]{2,1,0:T(1,128)S(1)}, f32[1,1,512]{2,1,0:T(1,128)}, u32[]{:S(2)}) copy-start(f32[1,1,512]{2,1,0:T(1,128)} %get-tuple-element.97) | copy-start | bytes 6148
  163.2 26.2 %copy-start.26 = (f32[1,1,512]{2,1,0:T(1,128)S(1)}, f32[1,1,512]{2,1,0:T(1,128)}, u32[]{:S(2)}) copy-start(f32[1,1,512]{2,1,0:T(1,128)} %get-tuple-element.100) | copy-start | bytes 6148
  163.2 26.2 %copy-start.27 = (f32[1,1,512]{2,1,0:T(1,128)S(1)}, f32[1,1,512]{2,1,0:T(1,128)}, u32[]{:S(2)}) copy-start(f32[1,1,512]{2,1,0:T(1,128)} %get-tuple-element.101) | copy-start | bytes 6148
  193.5 10.8 %copy-start.11 = (f32[386,512]{1,0:T(8,128)S(1)}, f32[386,512]{1,0:T(8,128)}, u32[]{:S(2)}) copy-start(f32[386,512]{1,0:T(8,128)} %convolution_add_fusion.2) | copy-start | bytes 2371588
  196.1 18.8 %copy-start.14 = (f32[32,64]{1,0:T(8,128)S(1)}, f32[32,64]{1,0:T(8,128)}, u32[]{:S(2)}) copy-start(f32[32,64]{1,0:T(8,128)} %get-tuple-element.103) | copy-start | bytes 24580
  196.1 18.8 %copy-start.15 = (f32[32,64]{1,0:T(8,128)S(1)}, f32[32,64]{1,0:T(8,128)}, u32[]{:S(2)}) copy-start(f32[32,64]{1,0:T(8,128)} %get-tuple-element.104) | copy-start | bytes 24580
  196.2 18.8 %copy-start.16 = (f32[32,64]{1,0:T(8,128)S(1)}, f32[32,64]{1,0:T(8,128)}, u32[]{:S(2)}) copy-start(f32[32,64]{1,0:T(8,128)} %get-tuple-element.105) | copy-start | bytes 24580
  196.2 18.9 %copy-start.4 = (f32[32,128,64]{1,2,0:T(8,128)S(1)}, f32[32,128,64]{1,2,0:T(8,128)}, u32[]{:S(2)}) copy-start(f32[32,128,64]{1,2,0:T(8,128)} %exponential_multiply_fusion) | copy-start | bytes 3145732
  196.2 18.9 %copy-start.13 = (f32[3,32,64,16]{2,3,1,0:T(8,128)S(1)}, f32[3,32,64,16]{2,3,1,0:T(8,128)}, u32[]{:S(2)}) copy-start(f32[3,32,64,16]{2,3,1,0:T(8,128)} %get-tuple-element.41) | copy-start | bytes 1179652
  196.2 10.7 %collective-permute-start.7 = (f32[32,64,16]{1,2,0:T(8,128)S(1)}, f32[32,64,16]{1,2,0:T(8,128)S(1)}, u32[]{:S(2)}, u32[]{:S(2)}) collective-permute-start(f32[32,64,16]{1,2,0:T(8,128)S(1)} %get-tuple-element.40), channel_id=1, source_target_pairs={{0,4},{4,8},{8,12},{1,5},{5,9},{9,13},{2,6},{6,10},{10,14},{3,7},{... | collective-permute-start | bytes 393224 | tf_op jit(solution)/shard_map/ppermute | solution.py:129
  199.8 11.5 %collective-permute-start.8 = (f32[32,64,16]{1,2,0:T(8,128)S(1)}, f32[32,64,16]{1,2,0:T(8,128)S(1)}, u32[]{:S(2)}, u32[]{:S(2)}) collective-permute-start(f32[32,64,16]{1,2,0:T(8,128)S(1)} %get-tuple-element.40), channel_id=1, source_target_pairs={{0,8},{4,12},{1,9},{5,13},{2,10},{6,14},{3,11},{7,15},{16,24},{20,... | collective-permute-start | bytes 393224 | tf_op jit(solution)/shard_map/ppermute | solution.py:129
  202.7 12.2 %collective-permute-start.9 = (f32[32,64,16]{1,2,0:T(8,128)S(1)}, f32[32,64,16]{1,2,0:T(8,128)S(1)}, u32[]{:S(2)}, u32[]{:S(2)}) collective-permute-start(f32[32,64,16]{1,2,0:T(8,128)S(1)} %get-tuple-element.40), channel_id=1, source_target_pairs={{0,12},{1,13},{2,14},{3,15},{16,28},{17,29},{18,30},{19,31}} | collective-permute-start | bytes 393224 | tf_op jit(solution)/shard_map/ppermute | solution.py:129
  206.9 9.4 %copy-start = (f32[32,128,128]{2,1,0:T(8,128)S(1)}, f32[32,128,128]{2,1,0:T(8,128)}, u32[]{:S(2)}) copy-start(f32[32,128,128]{2,1,0:T(8,128)} %slice.155) | copy-start | bytes 6291460
  220.4 28.6 %copy-start.2 = (bf16[384,1024]{1,0:T(8,128)(2,1)S(1)}, bf16[384,1024]{1,0:T(8,128)(2,1)}, u32[]{:S(2)}) copy-start(bf16[384,1024]{1,0:T(8,128)(2,1)} %param.9) | copy-start | bytes 2359300
  (11 other events, 33.9 us)
Sparse Core Ops, SparseCore 0:
  9.3 48.3 all-gather.9
  59.2 44.4 all-gather.11
  105.3 44.4 all-gather.13
  221.9 27.1 all-gather.7

commit v4 on v3

--- a/solution.py
+++ b/solution.py
@@ -99,9 +99,8 @@
         src_grp = (me_grp - by) % n_grp
         part = lax.dynamic_index_in_dim(normed4, src_grp, axis=2, keepdims=False)
         others.append((src_grp, jnp.roll(part, -me_ctx, axis=1)))
-    filtered = {}
-    for s in order:
-        got, received = relayed[s]
+    def project(s, received):
+        got = relayed[s][0]
         acc = jnp.einsum("tkr,krc->tc", mine, got, preferred_element_type=jnp.float32)
         for (src_grp, part), recv in zip(others, received):
             local = lax.dynamic_slice_in_dim(w_in[:, s, :], src_grp * piece, piece, axis=0)
@@ -109,9 +108,12 @@
             acc = acc + jnp.einsum(
                 "tkr,krc->tc", part[:, 1:], recv, preferred_element_type=jnp.float32
             )
-        filtered[s] = short_filter(acc.astype(jnp.bfloat16), short_taps[:, s, :], tok_rows)
+        rounded = lax.reduce_precision(acc, exponent_bits=8, mantissa_bits=7)
+        return short_filter(rounded, short_taps[:, s, :], tok_rows)
+
+    last = order[-1]
+    filtered = {s: project(s, relayed[s][1]) for s in order[:-1]}
     product = filtered[0] * filtered[2]
-    second = filtered[1]
     blocks = tok_rows // block_rows
     current = product.reshape(blocks, block_rows, local_groups, group_size)
     near = jnp.einsum("gij,bjgc->bigc", kernel, current, precision=highest)
@@ -133,6 +135,8 @@
     starts = lead * incoming[None] + local_starts
     distant = jnp.einsum("gin,bgnc->bigc", entry, starts, precision=highest)
     conv_out = (near + distant).reshape(tok_rows, local_width)
+    late, conv_out = lax.optimization_barrier((relayed[last][1], conv_out))
+    second = project(last, late)
     gated = (second * conv_out).astype(jnp.bfloat16)
     mixed = jnp.dot(
         lax.all_gather(gated, "tp", axis=1, tiled=True), w_out, preferred_element_type=jnp.float32

time: 265 us -> 245 us (0.925)
  waiting for transfers between devices: 125 us -> 104 us
  local copies, waits for them, and re-layouts: 47.7 us -> 50.4 us
    ppermute x3, waiting for transfers between devices: 25.4 us -> 0.01 us  [body(): received.append(lax.ppermute(send, 'grp', pairs))]
    all_gather x3, waiting for transfers between devices: 54 us -> 58.8 us  [body(): got = lax.all_gather(own[:, s, :], 'ctx', axis=0)]
  transfers between devices with their start and end apart: 14 -> 14, of which waited for: 8 -> 7; matrix products, arithmetic and copies ran while one was open for 33% -> 37% of each run, Pallas kernels for 0% -> 0%
where the time goes in v4:
time: 245 us; the launch traced here: 242 us
  waiting for transfers between devices  104 us (42%)
  local copies, waits for them, and re-layouts  50.4 us (21%)
  matrix products  29.6 us (12%)
  other arithmetic  24.6 us (10%)
  starting transfers between devices  19.1 us (8%)
  between operations  14 us (6%)
    all_gather x3, waiting for transfers between devices, body(): got = lax.all_gather(own[:, s, :], 'ctx', axis=0)  58.8 us
    all_gather x1, waiting for transfers between devices, body(): lax.all_gather(gated, 'tp', axis=1, tiled=True)  26.8 us
    reshape x1, local copies, waits for them, and re-layouts, banded(): tiled[:, :length * (2 * length - 1)]  9.44 us
    ppermute x3, waiting for transfers between devices, gather_by_permutes(): pieces.append(lax.ppermute(x, axis, pairs))  9.3 us
    concatenate x3, other arithmetic, body(): doubled = jnp.concatenate([got, got], axis=0)  8.95 us
    ppermute x3, waiting for transfers between devices, body(): arrived = lax.ppermute(own_state, 'ctx', pairs)  8.41 us
    dynamic_slice x1, local copies, waits for them, and re-layouts, body(): part = lax.dynamic_index_in_dim(normed4, src_grp, axis=2, keepdims=False)  8.27 us
    unnamed x67, local copies, waits for them, and re-layouts  7.86 us
  transfers between devices with their start and end apart: 14, of which 7 were waited for; matrix products, arithmetic and copies ran while one was open for 37% of the time, Pallas kernels for 0%

profile of v4, /device:TPU:0, one launch (start us, length us, event | category | flops | bytes accessed | tf_op | source)
XLA Modules:
  0.0 241.9 jit_solution(9429313478681606246)
XLA Ops:
  6.5 2.6 %constant_dynamic-slice_fusion.3 = (bf16[512,1,512]{2,0,1:T(8,128)(2,1)}, bf16[512,1,512]{2,0,1:T(8,128)(2,1)}, bf16[512,1,512]{2,0,1:T(8,128)(2,1)}) fusion(bf16[1024,3,512]{2,0,1:T(8,128)(2,1)} %param.11, s32[]{:T(128)S(6)} %select_n.52, s32[]{:T(128)S(6)} %add.178, s32[]{:T(128)S(6)} %add.177), kind=kLoop, calls=%fused_computation.111 | loop fusion | bytes 3145740 | tf_op jit(solution)/shard_map/slice | solution.py:75
  10.0 5.0 %collective-permute-start = (bf16[2,1024]{1,0:T(2,128)(2,1)S(1)}, bf16[2,1024]{1,0:T(2,128)(2,1)S(1)}, u32[]{:S(2)}, u32[]{:S(2)}) collective-permute-start(bf16[2,1024]{1,0:T(2,128)(2,1)S(1)} %slice.119), channel_id=1, source_target_pairs={{0,4},{4,8},{8,12},{1,5},{5,9},{9,13},{2,6},{6,10},{10,14},{3,7},{... | collective-permute-start | bytes 12296 | tf_op jit(solution)/shard_map/ppermute | solution.py:12
  15.1 3.6 %fusion.50 = (bf16[1024,1,512]{2,0,1:T(8,128)(2,1)}, bf16[1024,1,512]{2,0,1:T(8,128)(2,1)}, bf16[1024,1,512]{2,0,1:T(8,128)(2,1)}) fusion(bf16[1024,3,512]{2,0,1:T(8,128)(2,1)} %param.11), kind=kLoop, calls=%fused_computation.118 | loop fusion | bytes 6291456 | tf_op jit(solution)/shard_map/slice | solution.py:106
  29.6 2.4 %copy.32 = f32[4,8,128,256]{3,1,2,0:T(8,128)S(1)} copy(f32[4,8,128,256]{3,2,1,0:T(8,128)S(1)} %bitcast.145) | data formatting | bytes 8388608
  32.0 2.3 slice.151
  34.3 9.4 %reshape.91 = f32[32,128,255]{2,1,0:T(8,128)} reshape(f32[32,32640]{1,0:T(8,128)} %slice.151) | data formatting | bytes 8355840 | tf_op jit(solution)/shard_map/reshape | solution.py:29
  43.7 4.1 %slice.152 = f32[32,128,128]{2,1,0:T(8,128)} slice(f32[32,128,255]{2,1,0:T(8,128)} %reshape.91), slice={[0:32], [0:128], [127:255]} | slice | bytes 4194304 | tf_op jit(solution)/shard_map/slice | solution.py:67
  47.9 2.3 exponential_multiply_fusion
  50.3 7.5 %collective-permute-done.2 = bf16[387,1024]{1,0:T(8,128)(2,1)S(1)} collective-permute-done((bf16[387,1024]{1,0:T(8,128)(2,1)}, bf16[387,1024]{1,0:T(8,128)(2,1)S(1)}, u32[]{:S(2)}, u32[]{:S(2)}) %collective-permute-start.2) | collective-permute-done | bytes 792608 | tf_op jit(solution)/shard_map/ppermute | solution.py:38
  57.9 1.8 collective-permute-done.3
  62.4 2.7 %fusion.2 = bf16[386,4096]{1,0:T(8,128)(2,1)} fusion(f32[4096]{0:T(1024)S(1)} %bitcast.157, f32[386]{0:T(512)S(1)} %add_rsqrt_fusion, bf16[387,4096]{1,0:T(8,128)(2,1)S(1)} %pad_maximum_fusion), kind=kLoop, calls=%fused_computation.6 | loop fusion | flops 6324224 | bytes 6342152 | tf_op jit(solution)/shard_map/convert_element_type | solution.py:94
  65.2 7.4 %reshape.90 = bf16[386,4,2,512]{3,2,1,0:T(2,128)(2,1)S(1)} reshape(bf16[386,4096]{1,0:T(8,128)(2,1)} %fusion.2) | data formatting | bytes 6324224 | tf_op jit(solution)/shard_map/reshape | solution.py:95
  72.6 8.3 %constant_dynamic-slice_fusion.2 = (bf16[386,4,1,512]{3,2,1,0:T(2,128)(2,1)S(1)}, bf16[386,4,1,512]{3,2,1,0:T(2,128)(2,1)}) fusion(bf16[386,4,2,512]{3,2,1,0:T(2,128)(2,1)S(1)} %reshape.90, s32[]{:T(128)S(6)} %select_n.54, s32[]{:T(128)S(6)} %select_n.51), kind=kLoop, calls=%fused_computation.110 | loop fusion | bytes 6324232 | tf_op jit(solution)/shard_map/jit(dynamic_index_in_dim)/dynamic_slice | solution.py:100
  82.3 2.5 %fusion.7 = bf16[3,512,512]{2,1,0:T(8,128)(2,1)S(1)} fusion(s32[]{:T(128)S(6)} %select_n.58, bf16[4,512,512]{2,1,0:T(8,128)(2,1)} %bitcast.150), kind=kLoop, calls=%fused_computation.22 | loop fusion | flops 786432 | bytes 3670020 | tf_op jit(solution)/shard_map/concatenate | solution.py:78
  86.5 17.3 %all-gather.14.cloned.1.call-done = bf16[2048,1,512]{2,0,1:T(8,128)(2,1)} async-done(((bf16[512,1,512]{2,0,1:T(8,128)(2,1)}), bf16[2048,1,512]{2,0,1:T(8,128)(2,1)}) %all-gather.14.cloned.1.call-update) | async-done | bytes 2097168 | tf_op jit(solution)/shard_map/all_gather | solution.py:75
  103.8 3.1 %fusion.6 = bf16[3,512,512]{2,1,0:T(8,128)(2,1)} fusion(s32[]{:T(128)S(6)} %select_n.58, bf16[4,512,512]{2,1,0:T(8,128)(2,1)} %bitcast.152), kind=kLoop, calls=%fused_computation.21 | loop fusion | flops 786432 | bytes 3670020 | tf_op jit(solution)/shard_map/concatenate | solution.py:78
  108.4 41.5 %all-gather.10.cloned.1.call-done = bf16[2048,1,512]{2,0,1:T(8,128)(2,1)} async-done(((bf16[512,1,512]{2,0,1:T(8,128)(2,1)}), bf16[2048,1,512]{2,0,1:T(8,128)(2,1)}) %all-gather.10.cloned.1.call-update) | async-done | bytes 2097168 | tf_op jit(solution)/shard_map/all_gather | solution.py:75
  149.9 3.3 %fusion.8 = bf16[3,512,512]{2,1,0:T(8,128)(2,1)} fusion(s32[]{:T(128)S(6)} %select_n.58, bf16[4,512,512]{2,1,0:T(8,128)(2,1)} %bitcast.154), kind=kLoop, calls=%fused_computation.23 | loop fusion | flops 786432 | bytes 3670020 | tf_op jit(solution)/shard_map/concatenate | solution.py:78
  154.6 2.8 %convolution_bitcast_fusion.4 = f32[386,512]{1,0:T(8,128)S(1)} fusion(bf16[4,512,512]{2,1,0:T(8,128)(2,1)} %bitcast.151, bf16[386,4,1,512]{3,2,1,0:T(2,128)(2,1)S(1)} %copy-done.7), kind=kOutput, calls=%fused_computation.29 | convolution fusion | flops 809500672 | bytes 4468736 | tf_op jit(solution)/shard_map/tkr,krc->tc/dot_general | solution.py:104
  162.0 2.0 convolution_bitcast_fusion.5
  164.0 2.2 fusion.16
  166.3 2.2 fusion.18
  172.0 2.6 %while.13 = (s32[]{:T(128)}, f32[32,64,16]{1,2,0:T(8,128)S(1)}, f32[3,32,64,16]{2,3,1,0:T(8,128)}, f32[32,64,1]{1,0,2:T(8,128)S(1)}, f32[3,32,64,16]{2,3,0,1:T(8,128)S(1)}, /*index=5*/s32[]{:T(128)}, s32[]{:T(128)}) while((s32[]{:T(128)}, f32[32,64,16]{1,2,0:T(8,128)S(1)}, f32[3,32,64,16]{2,3,1,0:T(8,128)}, ...), condition=%wide.region_2.3_spmd.clone, body=%wide.region_1.2_spmd.clone.sunk | while | flops 131075 | bytes 795228 | solution.py:127
  174.6 2.2 collective-permute-start.7
  176.8 3.5 %collective-permute-start.8 = (f32[32,64,16]{1,2,0:T(8,128)S(1)}, f32[32,64,16]{1,2,0:T(8,128)S(1)}, u32[]{:S(2)}, u32[]{:S(2)}) collective-permute-start(f32[32,64,16]{1,2,0:T(8,128)S(1)} %get-tuple-element.42), channel_id=1, source_target_pairs={{0,8},{4,12},{1,9},{5,13},{2,10},{6,14},{3,11},{7,15},{16,24},{20,... | collective-permute-start | bytes 393224 | tf_op jit(solution)/shard_map/ppermute | solution.py:131
  181.9 2.5 %convolution_add_fusion.2 = f32[386,512]{1,0:T(8,128)} fusion(f32[386,512]{1,0:T(8,128)} %convolution_bitcast_fusion.5, bf16[1024,1,512]{2,0,1:T(8,128)(2,1)S(1)} %copy-done.8, s32[]{:T(128)S(6)} %select_n.57, bf16[386,4,512]{2,0,1:T(8,128)(2,1)} %copy-done.3), kind=kOutput, calls=%fused_computation.33 | convolution fusion | flops 202572800 | bytes 2519044 | tf_op jit(solution)/shard_map/dot_general | solution.py:107
  184.4 4.6 %collective-permute-done.8 = f32[32,64,16]{1,2,0:T(8,128)S(1)} collective-permute-done((f32[32,64,16]{1,2,0:T(8,128)S(1)}, f32[32,64,16]{1,2,0:T(8,128)S(1)}, u32[]{:S(2)}, u32[]{:S(2)}) %collective-permute-start.8) | collective-permute-done | bytes 131104 | tf_op jit(solution)/shard_map/ppermute | solution.py:131
  189.0 3.9 %collective-permute-done.9 = f32[32,64,16]{1,2,0:T(8,128)S(1)} collective-permute-done((f32[32,64,16]{1,2,0:T(8,128)S(1)}, f32[32,64,16]{1,2,0:T(8,128)S(1)}, u32[]{:S(2)}, u32[]{:S(2)}) %collective-permute-start.9) | collective-permute-done | bytes 131104 | tf_op jit(solution)/shard_map/ppermute | solution.py:131
  194.2 3.4 %fusion.12 = f32[3,128,32,16]{1,3,0,2:T(8,128)S(1)} fusion(f32[32,3,16,128]{3,2,1,0:T(8,128)S(1)} %fusion.21, f32[32,128,128]{2,1,0:T(8,128)S(1)} %copy-done, f32[3,128,32,16]{1,0,3,2:T(4,128)S(1)} %reshape.92), kind=kOutput, calls=%fused_computation.35 | convolution fusion | flops 302186496 | bytes 4456448 | tf_op jit(solution)/shard_map/gij,bjgc->bigc/dot_general | solution.py:119
  199.4 2.4 fusion.20
  202.9 26.8 %all-gather.8.cloned.1.call-done = bf16[384,2048]{1,0:T(8,128)(2,1)} async-done(((bf16[384,512]{1,0:T(8,128)(2,1)}), bf16[384,2048]{1,0:T(8,128)(2,1)}) %all-gather.8.cloned.1.call-update) | async-done | bytes 1572880 | tf_op jit(solution)/shard_map/all_gather | solution.py:142
  229.7 5.3 %add_convert_fusion = bf16[384,1024]{1,0:T(8,128)(2,1)} fusion(bf16[384,1024]{1,0:T(8,128)(2,1)S(1)} %copy-done.2, bf16[384,2048]{1,0:T(8,128)(2,1)} %all-gather.8.cloned.1.call-done, bf16[2048,1024]{1,0:T(8,128)(2,1)} %param.15), kind=kOutput, calls=%fused_computation.24 | convolution fusion | flops 1611792384 | bytes 7340032 | tf_op jit(solution)/shard_map/dot_general | solution.py:141
  (131 shorter events, 36.8 us)
Async XLA Ops:
  6.5 75.8 %all-gather.12.cloned.1.call-start = ((), (), s32[]{:S(2)}) async-start(), calls=%async_computation.2 | async-start | bytes 2621440 | tf_op jit(solution)/shard_map/all_gather | solution.py:75
  6.5 3.5 %copy-start.1 = (bf16[384,1024]{1,0:T(8,128)(2,1)S(1)}, bf16[384,1024]{1,0:T(8,128)(2,1)}, u32[]{:S(2)}) copy-start(bf16[384,1024]{1,0:T(8,128)(2,1)} %param.9) | copy-start | bytes 2359300
  9.2 94.6 %all-gather.14.cloned.1.call-start = ((), (), s32[]{:S(2)}) async-start(), calls=%async_computation.3 | async-start | bytes 2621440 | tf_op jit(solution)/shard_map/all_gather | solution.py:75
  10.0 139.9 %all-gather.10.cloned.1.call-start = ((), (), s32[]{:S(2)}) async-start(), calls=%async_computation.1 | async-start | bytes 2621440 | tf_op jit(solution)/shard_map/all_gather | solution.py:75
  10.0 10.8 %collective-permute-start = (bf16[2,1024]{1,0:T(2,128)(2,1)S(1)}, bf16[2,1024]{1,0:T(2,128)(2,1)S(1)}, u32[]{:S(2)}, u32[]{:S(2)}) collective-permute-start(bf16[2,1024]{1,0:T(2,128)(2,1)S(1)} %slice.119), channel_id=1, source_target_pairs={{0,4},{4,8},{8,12},{1,5},{5,9},{9,13},{2,6},{6,10},{10,14},{3,7},{... | collective-permute-start | bytes 12296 | tf_op jit(solution)/shard_map/ppermute | solution.py:12
  15.0 3.7 %copy-start.18 = (f32[32,64]{1,0:T(8,128)S(1)}, f32[32,64]{1,0:T(8,128)}, u32[]{:S(2)}) copy-start(f32[32,64]{1,0:T(8,128)} %param.13) | copy-start | bytes 24580
  15.0 3.7 %copy-start.19 = (f32[32,64]{1,0:T(8,128)S(1)}, f32[32,64]{1,0:T(8,128)}, u32[]{:S(2)}) copy-start(f32[32,64]{1,0:T(8,128)} %param.14) | copy-start | bytes 24580
  15.0 5.8 %copy-start.28 = (bf16[1024]{0:T(1024)(128)(2,1)S(1)}, bf16[1024]{0:T(1024)(128)(2,1)}, u32[]{:S(2)}) copy-start(bf16[1024]{0:T(1024)(128)(2,1)} %param.10) | copy-start | bytes 6148
  15.1 214.7 %all-gather.8.cloned.1.call-start = ((), (), s32[]{:S(2)}) async-start(), calls=%async_computation | async-start | bytes 1966080 | tf_op jit(solution)/shard_map/all_gather | solution.py:142
  18.7 6.5 %copy-start.20 = (f32[3,3,512]{2,1,0:T(4,128)S(1)}, f32[3,3,512]{2,1,0:T(4,128)}, u32[]{:S(2)}) copy-start(f32[3,3,512]{2,1,0:T(4,128)} %param.12) | copy-start | bytes 55300
  19.4 3.2 %copy-start.17 = (f32[32,64]{1,0:T(8,128)}, f32[32,64]{1,0:T(8,128)S(1)}, u32[]{:S(2)}) copy-start(f32[32,64]{1,0:T(8,128)S(1)} %get-tuple-element.112) | copy-start | bytes 24580
  22.0 28.2 %collective-permute-start.1 = (bf16[387,1024]{1,0:T(8,128)(2,1)}, bf16[387,1024]{1,0:T(8,128)(2,1)S(1)}, u32[]{:S(2)}, u32[]{:S(2)}) collective-permute-start(bf16[387,1024]{1,0:T(8,128)(2,1)} %pad_maximum_fusion.1), channel_id=1, source_target_pairs={{0,3},{1,0},{2,1},{3,2},{4,7},{5,4},{6,5},{7,6},{8,11},{9,8},{10,9... | collective-permute-start | bytes 2377736 | tf_op jit(solution)/shard_map/ppermute | solution.py:38
  24.3 33.5 %collective-permute-start.2 = (bf16[387,1024]{1,0:T(8,128)(2,1)}, bf16[387,1024]{1,0:T(8,128)(2,1)S(1)}, u32[]{:S(2)}, u32[]{:S(2)}) collective-permute-start(bf16[387,1024]{1,0:T(8,128)(2,1)} %pad_maximum_fusion.1), channel_id=1, source_target_pairs={{0,2},{1,3},{2,0},{3,1},{4,6},{5,7},{6,4},{7,5},{8,10},{9,11},{10,... | collective-permute-start | bytes 2377736 | tf_op jit(solution)/shard_map/ppermute | solution.py:38
  25.8 33.8 %collective-permute-start.3 = (bf16[387,1024]{1,0:T(8,128)(2,1)}, bf16[387,1024]{1,0:T(8,128)(2,1)S(1)}, u32[]{:S(2)}, u32[]{:S(2)}) collective-permute-start(bf16[387,1024]{1,0:T(8,128)(2,1)} %pad_maximum_fusion.1), channel_id=1, source_target_pairs={{0,1},{1,2},{2,3},{3,0},{4,5},{5,6},{6,7},{7,4},{8,9},{9,10},{10,1... | collective-permute-start | bytes 2377736 | tf_op jit(solution)/shard_map/ppermute | solution.py:38
  82.3 83.9 %copy-start.3 = (bf16[386,4,512]{2,0,1:T(8,128)(2,1)}, bf16[386,4,512]{2,0,1:T(8,128)(2,1)S(1)}, u32[]{:S(2)}) copy-start(bf16[386,4,512]{2,0,1:T(8,128)(2,1)S(1)} %fusion.5) | copy-start | bytes 4743172
  84.9 79.1 %collective-permute-start.5 = (bf16[3,512,512]{2,1,0:T(8,128)(2,1)S(1)}, bf16[3,512,512]{2,1,0:T(8,128)(2,1)}, u32[]{:S(2)}, u32[]{:S(2)}) collective-permute-start(bf16[3,512,512]{2,1,0:T(8,128)(2,1)S(1)} %fusion.7), channel_id=1, source_target_pairs={{0,16},{16,0},{1,17},{17,1},{2,18},{18,2},{3,19},{19,3},{4,20},{20... | collective-permute-start | bytes 4718600 | tf_op jit(solution)/shard_map/ppermute | solution.py:83
  106.9 59.3 %collective-permute-start.6 = (bf16[3,512,512]{2,1,0:T(8,128)(2,1)}, bf16[3,512,512]{2,1,0:T(8,128)(2,1)}, u32[]{:S(2)}, u32[]{:S(2)}) collective-permute-start(bf16[3,512,512]{2,1,0:T(8,128)(2,1)} %fusion.6), channel_id=1, source_target_pairs={{0,16},{16,0},{1,17},{17,1},{2,18},{18,2},{3,19},{19,3},{4,20},{20... | collective-permute-start | bytes 4718600 | tf_op jit(solution)/shard_map/ppermute | solution.py:83
  149.9 4.8 %copy-start.7 = (bf16[386,4,1,512]{3,2,1,0:T(2,128)(2,1)S(1)}, bf16[386,4,1,512]{3,2,1,0:T(2,128)(2,1)}, u32[]{:S(2)}) copy-start(bf16[386,4,1,512]{3,2,1,0:T(2,128)(2,1)} %get-tuple-element.90) | copy-start | bytes 4743172
  153.1 44.9 %collective-permute-start.4 = (bf16[3,512,512]{2,1,0:T(8,128)(2,1)}, bf16[3,512,512]{2,1,0:T(8,128)(2,1)}, u32[]{:S(2)}, u32[]{:S(2)}) collective-permute-start(bf16[3,512,512]{2,1,0:T(8,128)(2,1)} %fusion.8), channel_id=1, source_target_pairs={{0,16},{16,0},{1,17},{17,1},{2,18},{18,2},{3,19},{19,3},{4,20},{20... | collective-permute-start | bytes 4718600 | tf_op jit(solution)/shard_map/ppermute | solution.py:83
  154.6 2.8 %copy-start.10 = (bf16[1024,1,512]{2,0,1:T(8,128)(2,1)S(1)}, bf16[1024,1,512]{2,0,1:T(8,128)(2,1)}, u32[]{:S(2)}) copy-start(bf16[1024,1,512]{2,0,1:T(8,128)(2,1)} %get-tuple-element.93) | copy-start | bytes 3145732
  172.0 9.9 %copy-start.8 = (bf16[1024,1,512]{2,0,1:T(8,128)(2,1)S(1)}, bf16[1024,1,512]{2,0,1:T(8,128)(2,1)}, u32[]{:S(2)}) copy-start(bf16[1024,1,512]{2,0,1:T(8,128)(2,1)} %get-tuple-element.91) | copy-start | bytes 3145732
  174.6 18.3 %copy-start.14 = (f32[32,64]{1,0:T(8,128)S(1)}, f32[32,64]{1,0:T(8,128)}, u32[]{:S(2)}) copy-start(f32[32,64]{1,0:T(8,128)} %get-tuple-element.107) | copy-start | bytes 24580
  174.6 18.3 %copy-start.15 = (f32[32,64]{1,0:T(8,128)S(1)}, f32[32,64]{1,0:T(8,128)}, u32[]{:S(2)}) copy-start(f32[32,64]{1,0:T(8,128)} %get-tuple-element.108) | copy-start | bytes 24580
  174.6 18.2 %copy-start.16 = (f32[32,64]{1,0:T(8,128)S(1)}, f32[32,64]{1,0:T(8,128)}, u32[]{:S(2)}) copy-start(f32[32,64]{1,0:T(8,128)} %get-tuple-element.109) | copy-start | bytes 24580
  174.6 18.3 %copy-start.6 = (f32[32,128,64]{1,2,0:T(8,128)S(1)}, f32[32,128,64]{1,2,0:T(8,128)}, u32[]{:S(2)}) copy-start(f32[32,128,64]{1,2,0:T(8,128)} %exponential_multiply_fusion) | copy-start | bytes 3145732
  174.6 18.3 %copy-start.13 = (f32[3,32,64,16]{2,3,1,0:T(8,128)S(1)}, f32[3,32,64,16]{2,3,1,0:T(8,128)}, u32[]{:S(2)}) copy-start(f32[3,32,64,16]{2,3,1,0:T(8,128)} %get-tuple-element.43) | copy-start | bytes 1179652
  174.6 9.8 %collective-permute-start.7 = (f32[32,64,16]{1,2,0:T(8,128)S(1)}, f32[32,64,16]{1,2,0:T(8,128)S(1)}, u32[]{:S(2)}, u32[]{:S(2)}) collective-permute-start(f32[32,64,16]{1,2,0:T(8,128)S(1)} %get-tuple-element.42), channel_id=1, source_target_pairs={{0,4},{4,8},{8,12},{1,5},{5,9},{9,13},{2,6},{6,10},{10,14},{3,7},{... | collective-permute-start | bytes 393224 | tf_op jit(solution)/shard_map/ppermute | solution.py:131
  176.8 12.2 %collective-permute-start.8 = (f32[32,64,16]{1,2,0:T(8,128)S(1)}, f32[32,64,16]{1,2,0:T(8,128)S(1)}, u32[]{:S(2)}, u32[]{:S(2)}) collective-permute-start(f32[32,64,16]{1,2,0:T(8,128)S(1)} %get-tuple-element.42), channel_id=1, source_target_pairs={{0,8},{4,12},{1,9},{5,13},{2,10},{6,14},{3,11},{7,15},{16,24},{20,... | collective-permute-start | bytes 393224 | tf_op jit(solution)/shard_map/ppermute | solution.py:131
  180.3 12.5 %collective-permute-start.9 = (f32[32,64,16]{1,2,0:T(8,128)S(1)}, f32[32,64,16]{1,2,0:T(8,128)S(1)}, u32[]{:S(2)}, u32[]{:S(2)}) collective-permute-start(f32[32,64,16]{1,2,0:T(8,128)S(1)} %get-tuple-element.42), channel_id=1, source_target_pairs={{0,12},{1,13},{2,14},{3,15},{16,28},{17,29},{18,30},{19,31}} | collective-permute-start | bytes 393224 | tf_op jit(solution)/shard_map/ppermute | solution.py:131
  184.4 9.7 %copy-start = (f32[32,128,128]{2,1,0:T(8,128)S(1)}, f32[32,128,128]{2,1,0:T(8,128)}, u32[]{:S(2)}) copy-start(f32[32,128,128]{2,1,0:T(8,128)} %slice.152) | copy-start | bytes 6291460
  199.4 2.4 %copy-start.21 = (f32[1,1,512]{2,1,0:T(1,128)S(1)}, f32[1,1,512]{2,1,0:T(1,128)}, u32[]{:S(2)}) copy-start(f32[1,1,512]{2,1,0:T(1,128)} %get-tuple-element.105) | copy-start | bytes 6148
  201.8 27.9 %copy-start.2 = (bf16[384,1024]{1,0:T(8,128)(2,1)S(1)}, bf16[384,1024]{1,0:T(8,128)(2,1)}, u32[]{:S(2)}) copy-start(bf16[384,1024]{1,0:T(8,128)(2,1)} %param.9) | copy-start | bytes 2359300
  (11 other events, 20.9 us)
Sparse Core Ops, SparseCore 0:
  9.3 48.4 all-gather.11
  59.4 44.4 all-gather.13
  105.4 44.4 all-gather.9
  203.0 26.6 all-gather.7

commit v5 on v4

--- a/solution.py
+++ b/solution.py
@@ -38,6 +38,28 @@
         pieces.append(lax.ppermute(x, axis, pairs))
     stacked = jnp.stack(pieces[::-1], axis=0)
     return jnp.roll(stacked, me + 1, axis=0)
+
+
+def gather_by_swaps(x, axis):
+    count = lax.axis_size(axis)
+    me = lax.axis_index(axis)
+    bits = []
+    b = 1
+    while b < count:
+        bits.append(b)
+        b *= 2
+    if 2 ** len(bits) != count:
+        return lax.all_gather(x, axis, axis=0)
+    held = x[None]
+    masks = [0]
+    for bit in bits[::-1]:
+        pairs = [(q, q ^ bit) for q in range(count)]
+        held = jnp.concatenate([held, lax.ppermute(held, axis, pairs)], axis=0)
+        masks = masks + [m ^ bit for m in masks]
+    inverse = [masks.index(m) for m in range(count)]
+    table = jnp.array(inverse, jnp.int32)
+    where = jnp.take(table, jnp.bitwise_xor(jnp.arange(count, dtype=jnp.int32), me))
+    return jnp.take(held, where, axis=0)
 
 
 def body(tokens, norm_gain, w_in, short_taps, rates, residues, w_out):
@@ -138,9 +160,9 @@
     late, conv_out = lax.optimization_barrier((relayed[last][1], conv_out))
     second = project(last, late)
     gated = (second * conv_out).astype(jnp.bfloat16)
-    mixed = jnp.dot(
-        lax.all_gather(gated, "tp", axis=1, tiled=True), w_out, preferred_element_type=jnp.float32
-    )
+    pieces = gather_by_swaps(gated, "tp")
+    mixed = jnp.einsum("qtc,qcf->tf", pieces, w_out.reshape(pieces.shape[0], local_width, -1),
+                       preferred_element_type=jnp.float32)
     return (tokens.astype(jnp.float32) + mixed).astype(jnp.bfloat16)
 
 

time: 245 us -> 237 us (0.967)
  the two profiles are of different devices: /device:TPU:0 before, /device:TPU:25 now
where the time goes in v5:
time: 237 us; the launch traced here: 234 us
  waiting for transfers between devices  96.6 us (41%)
  local copies, waits for them, and re-layouts  52.8 us (22%)
  matrix products  29.7 us (13%)
  other arithmetic  24.1 us (10%)
  starting transfers between devices  16.7 us (7%)
  between operations  14.1 us (6%)
    all_gather x3, waiting for transfers between devices, body(): got = lax.all_gather(own[:, s, :], 'ctx', axis=0)  60.5 us
    ppermute x3, waiting for transfers between devices, body(): arrived = lax.ppermute(own_state, 'ctx', pairs)  19.5 us
    reshape x1, local copies, waits for them, and re-layouts, banded(): tiled[:, :length * (2 * length - 1)]  9.44 us
    concatenate x3, other arithmetic, body(): doubled = jnp.concatenate([got, got], axis=0)  8.95 us
    ppermute x2, waiting for transfers between devices, gather_by_swaps(): held = jnp.concatenate([held, lax.ppermute(held, axis, pairs)], axis=0)  8.71 us
    dynamic_slice x1, local copies, waits for them, and re-layouts, body(): part = lax.dynamic_index_in_dim(normed4, src_grp, axis=2, keepdims=False)  8.27 us
    unnamed x69, local copies, waits for them, and re-layouts  7.87 us
    reshape x1, local copies, waits for them, and re-layouts, body(): normed4 = normed.reshape(ext_rows, n_ctx, n_grp, piece)  7.4 us
  transfers between devices with their start and end apart: 15, of which 7 were waited for; matrix products, arithmetic and copies ran while one was open for 38% of the time, Pallas kernels for 0%

profile of v5, /device:TPU:25, one launch (start us, length us, event | category | flops | bytes accessed | tf_op | source)
XLA Modules:
  0.0 233.9 jit_solution(8335344822123958115)
XLA Ops:
  6.5 2.6 %constant_dynamic-slice_fusion.3 = (bf16[512,1,512]{2,0,1:T(8,128)(2,1)}, bf16[512,1,512]{2,0,1:T(8,128)(2,1)}, bf16[512,1,512]{2,0,1:T(8,128)(2,1)}) fusion(bf16[1024,3,512]{2,0,1:T(8,128)(2,1)} %param.12, s32[]{:T(128)S(6)} %select_n.112, s32[]{:T(128)S(6)} %add.218, s32[]{:T(128)S(6)} %add.217), kind=kLoop, calls=%fused_computation.121 | loop fusion | bytes 3145740 | tf_op jit(solution)/shard_map/slice | solution.py:97
  11.4 3.6 %fusion.61 = (bf16[1024,1,512]{2,0,1:T(8,128)(2,1)}, bf16[1024,1,512]{2,0,1:T(8,128)(2,1)}, bf16[1024,1,512]{2,0,1:T(8,128)(2,1)}) fusion(bf16[1024,3,512]{2,0,1:T(8,128)(2,1)} %param.12), kind=kLoop, calls=%fused_computation.140 | loop fusion | bytes 6291456 | tf_op jit(solution)/shard_map/slice | solution.py:128
  18.9 1.7 fusion.30
  22.5 1.9 collective-permute-start.3
  27.4 2.4 %copy.33 = f32[4,8,128,256]{3,1,2,0:T(8,128)S(1)} copy(f32[4,8,128,256]{3,2,1,0:T(8,128)S(1)} %bitcast.159) | data formatting | bytes 8388608
  29.8 2.3 slice.155
  32.1 9.4 %reshape.147 = f32[32,128,255]{2,1,0:T(8,128)} reshape(f32[32,32640]{1,0:T(8,128)} %slice.155) | data formatting | bytes 8355840 | tf_op jit(solution)/shard_map/reshape | solution.py:29
  41.5 4.1 %slice.156 = f32[32,128,128]{2,1,0:T(8,128)} slice(f32[32,128,255]{2,1,0:T(8,128)} %reshape.147), slice={[0:32], [0:128], [127:255]} | slice | bytes 4194304 | tf_op jit(solution)/shard_map/slice | solution.py:89
  45.6 2.3 %exponential_multiply_fusion = f32[32,128,64]{1,2,0:T(8,128)} fusion(f32[128]{0:T(128)} %broadcast_add_fusion, f32[32,64]{1,0:T(8,128)S(1)} %get-tuple-element.111, f32[32,64]{1,0:T(8,128)} %copy-done.18), kind=kLoop, calls=%fused_computation.53 | loop fusion | flops 524288 | bytes 1065472 | tf_op jit(solution)/shard_map/mul | solution.py:91
  48.1 7.1 %collective-permute-done.3 = bf16[387,1024]{1,0:T(8,128)(2,1)S(1)} collective-permute-done((bf16[387,1024]{1,0:T(8,128)(2,1)}, bf16[387,1024]{1,0:T(8,128)(2,1)S(1)}, u32[]{:S(2)}, u32[]{:S(2)}) %collective-permute-start.3) | collective-permute-done | bytes 792608 | tf_op jit(solution)/shard_map/ppermute | solution.py:38
  58.0 2.7 %fusion.2 = bf16[386,4096]{1,0:T(8,128)(2,1)} fusion(f32[4096]{0:T(1024)S(1)} %bitcast.171, f32[386]{0:T(512)S(1)} %add_rsqrt_fusion, bf16[387,4096]{1,0:T(8,128)(2,1)S(1)} %pad_maximum_fusion), kind=kLoop, calls=%fused_computation.8 | loop fusion | flops 6324224 | bytes 6342152 | tf_op jit(solution)/shard_map/convert_element_type | solution.py:116
  60.7 7.4 %reshape.146 = bf16[386,4,2,512]{3,2,1,0:T(2,128)(2,1)S(1)} reshape(bf16[386,4096]{1,0:T(8,128)(2,1)} %fusion.2) | data formatting | bytes 6324224 | tf_op jit(solution)/shard_map/reshape | solution.py:117
  68.1 8.3 %constant_dynamic-slice_fusion.2 = (bf16[386,4,1,512]{3,2,1,0:T(2,128)(2,1)S(1)}, bf16[386,4,1,512]{3,2,1,0:T(2,128)(2,1)}) fusion(bf16[386,4,2,512]{3,2,1,0:T(2,128)(2,1)S(1)} %reshape.146, s32[]{:T(128)S(6)} %select_n.114, s32[]{:T(128)S(6)} %select_n.111), kind=kLoop, calls=%fused_computation.120 | loop fusion | bytes 6324232 | tf_op jit(solution)/shard_map/jit(dynamic_index_in_dim)/dynamic_slice | solution.py:122
  77.9 2.5 %fusion.7 = bf16[3,512,512]{2,1,0:T(8,128)(2,1)S(1)} fusion(s32[]{:T(128)S(6)} %select_n.118, bf16[4,512,512]{2,1,0:T(8,128)(2,1)} %bitcast.164), kind=kLoop, calls=%fused_computation.24 | loop fusion | flops 786432 | bytes 3670020 | tf_op jit(solution)/shard_map/concatenate | solution.py:100
  81.8 18.5 %all-gather.11.cloned.1.call-done = bf16[2048,1,512]{2,0,1:T(8,128)(2,1)} async-done(((bf16[512,1,512]{2,0,1:T(8,128)(2,1)}), bf16[2048,1,512]{2,0,1:T(8,128)(2,1)}) %all-gather.11.cloned.1.call-update) | async-done | bytes 2097168 | tf_op jit(solution)/shard_map/all_gather | solution.py:97
  100.3 3.1 %fusion.6 = bf16[3,512,512]{2,1,0:T(8,128)(2,1)} fusion(s32[]{:T(128)S(6)} %select_n.118, bf16[4,512,512]{2,1,0:T(8,128)(2,1)} %bitcast.166), kind=kLoop, calls=%fused_computation.23 | loop fusion | flops 786432 | bytes 3670020 | tf_op jit(solution)/shard_map/concatenate | solution.py:100
  104.3 42.0 %all-gather.7.cloned.1.call-done = bf16[2048,1,512]{2,0,1:T(8,128)(2,1)} async-done(((bf16[512,1,512]{2,0,1:T(8,128)(2,1)}), bf16[2048,1,512]{2,0,1:T(8,128)(2,1)}) %all-gather.7.cloned.1.call-update) | async-done | bytes 2097168 | tf_op jit(solution)/shard_map/all_gather | solution.py:97
  146.3 3.3 %fusion.8 = bf16[3,512,512]{2,1,0:T(8,128)(2,1)} fusion(s32[]{:T(128)S(6)} %select_n.118, bf16[4,512,512]{2,1,0:T(8,128)(2,1)} %bitcast.168), kind=kLoop, calls=%fused_computation.25 | loop fusion | flops 786432 | bytes 3670020 | tf_op jit(solution)/shard_map/concatenate | solution.py:100
  150.5 2.8 %convolution_bitcast_fusion.4 = f32[386,512]{1,0:T(8,128)S(1)} fusion(bf16[4,512,512]{2,1,0:T(8,128)(2,1)} %bitcast.165, bf16[386,4,1,512]{3,2,1,0:T(2,128)(2,1)S(1)} %copy-done.8), kind=kOutput, calls=%fused_computation.36 | convolution fusion | flops 809500672 | bytes 4468736 | tf_op jit(solution)/shard_map/tkr,krc->tc/dot_general | solution.py:126
  157.9 2.0 convolution_bitcast_fusion.5
  159.9 2.2 fusion.22
  162.2 2.2 fusion.24
  167.9 2.6 %while.13 = (s32[]{:T(128)}, f32[32,64,16]{1,2,0:T(8,128)S(1)}, f32[3,32,64,16]{2,3,1,0:T(8,128)}, f32[32,64,1]{1,0,2:T(8,128)S(1)}, f32[3,32,64,16]{2,3,0,1:T(8,128)S(1)}, /*index=5*/s32[]{:T(128)}, s32[]{:T(128)}) while((s32[]{:T(128)}, f32[32,64,16]{1,2,0:T(8,128)S(1)}, f32[3,32,64,16]{2,3,1,0:T(8,128)}, ...), condition=%wide.region_2.3_spmd.clone, body=%wide.region_1.2_spmd.clone.sunk | while | flops 131075 | bytes 795228 | solution.py:149
  174.8 2.5 %convolution_add_fusion.2 = f32[386,512]{1,0:T(8,128)} fusion(f32[386,512]{1,0:T(8,128)} %convolution_bitcast_fusion.5, bf16[1024,1,512]{2,0,1:T(8,128)(2,1)S(1)} %copy-done.9, s32[]{:T(128)S(6)} %select_n.117, bf16[386,4,512]{2,0,1:T(8,128)(2,1)} %copy-done.4), kind=kOutput, calls=%fused_computation.40 | convolution fusion | flops 202572800 | bytes 2519044 | tf_op jit(solution)/shard_map/dot_general | solution.py:129
  177.4 2.3 %collective-permute-done.7 = f32[32,64,16]{1,2,0:T(8,128)S(1)} collective-permute-done((f32[32,64,16]{1,2,0:T(8,128)S(1)}, f32[32,64,16]{1,2,0:T(8,128)S(1)}, u32[]{:S(2)}, u32[]{:S(2)}) %collective-permute-start.7) | collective-permute-done | bytes 131104 | tf_op jit(solution)/shard_map/ppermute | solution.py:153
  179.7 17.1 %collective-permute-done.8 = f32[32,64,16]{1,2,0:T(8,128)S(1)} collective-permute-done((f32[32,64,16]{1,2,0:T(8,128)S(1)}, f32[32,64,16]{1,2,0:T(8,128)S(1)}, u32[]{:S(2)}, u32[]{:S(2)}) %collective-permute-start.8) | collective-permute-done | bytes 131104 | tf_op jit(solution)/shard_map/ppermute | solution.py:153
  198.2 3.4 %fusion.18 = f32[3,128,32,16]{1,3,0,2:T(8,128)S(1)} fusion(f32[32,3,16,128]{3,2,1,0:T(8,128)S(1)} %fusion.27, f32[32,128,128]{2,1,0:T(8,128)S(1)} %copy-done.1, f32[3,128,32,16]{1,0,3,2:T(4,128)S(1)} %reshape.148), kind=kOutput, calls=%fused_computation.42 | convolution fusion | flops 302186496 | bytes 4456448 | tf_op jit(solution)/shard_map/gij,bjgc->bigc/dot_general | solution.py:141
  203.4 2.4 %fusion.26 = f32[386,512]{1,0:T(8,128)S(1)} fusion(f32[386,512]{1,0:T(8,128)} %convolution_add_fusion.2, bf16[386,4,512]{2,0,1:T(8,128)(2,1)S(1)} %copy-done.5, bf16[3,512,512]{2,1,0:T(8,128)(2,1)} %collective-permute-done.4), kind=kOutput, calls=%fused_computation.49 | convolution fusion | flops 607520768 | bytes 4734976 | tf_op jit(solution)/shard_map/tkr,krc->tc/dot_general | solution.py:130
  207.4 7.5 %collective-permute-done.10 = bf16[1,384,512]{2,1,0:T(8,128)(2,1)S(1)} collective-permute-done((bf16[1,384,512]{2,1,0:T(8,128)(2,1)S(1)}, bf16[1,384,512]{2,1,0:T(8,128)(2,1)S(1)}, u32[]{:S(2)}, u32[]{:S(2)}) %collective-permute-start.10) | collective-permute-done | bytes 393248 | tf_op jit(solution)/shard_map/ppermute | solution.py:57
  215.0 2.9 %collective-permute-start.11 = (bf16[2,384,512]{2,1,0:T(8,128)(2,1)S(1)}, bf16[2,384,512]{2,1,0:T(8,128)(2,1)S(1)}, u32[]{:S(2)}, u32[]{:S(2)}) collective-permute-start(bf16[2,384,512]{2,1,0:T(8,128)(2,1)S(1)} %pad_maximum_fusion.3), channel_id=1, source_target_pairs={{0,1},{1,0},{2,3},{3,2},{4,5},{5,4},{6,7},{7,6},{8,9},{9,8},{10,11... | collective-permute-start | bytes 2359304 | tf_op jit(solution)/shard_map/ppermute | solution.py:57
  219.9 1.8 gather_fusion.1
  221.8 5.4 %fusion.9 = bf16[384,1024]{1,0:T(8,128)(2,1)} fusion(bf16[384,1024]{1,0:T(8,128)(2,1)S(1)} %copy-done.3, bf16[4,512,1024]{2,1,0:T(8,128)(2,1)} %bitcast.183, bf16[4,384,512]{2,1,0:T(8,128)(2,1)} %gather_fusion.1, pred[4]{0:T(512)(128)(4,1)S(1)} %compare_and_fusion), kind=kOutput, calls=%fused_computation.28 | convolution fusion | flops 1612578816 | bytes 7340036 | tf_op jit(solution)/shard_map/qtc,qcf->tf/dot_general | solution.py:164
  (143 shorter events, 39.8 us)
Async XLA Ops:
  6.5 71.4 %all-gather.9.cloned.1.call-start = ((), (), s32[]{:S(2)}) async-start(), calls=%async_computation.1 | async-start | bytes 2621440 | tf_op jit(solution)/shard_map/all_gather | solution.py:97
  6.5 3.5 %copy-start.2 = (bf16[384,1024]{1,0:T(8,128)(2,1)S(1)}, bf16[384,1024]{1,0:T(8,128)(2,1)}, u32[]{:S(2)}) copy-start(bf16[384,1024]{1,0:T(8,128)(2,1)} %param.10) | copy-start | bytes 2359300
  9.2 91.1 %all-gather.11.cloned.1.call-start = ((), (), s32[]{:S(2)}) async-start(), calls=%async_computation.2 | async-start | bytes 2621440 | tf_op jit(solution)/shard_map/all_gather | solution.py:97
  10.0 136.4 %all-gather.7.cloned.1.call-start = ((), (), s32[]{:S(2)}) async-start(), calls=%async_computation | async-start | bytes 2621440 | tf_op jit(solution)/shard_map/all_gather | solution.py:97
  10.0 7.1 %collective-permute-start = (bf16[2,1024]{1,0:T(2,128)(2,1)S(1)}, bf16[2,1024]{1,0:T(2,128)(2,1)S(1)}, u32[]{:S(2)}, u32[]{:S(2)}) collective-permute-start(bf16[2,1024]{1,0:T(2,128)(2,1)S(1)} %slice.119), channel_id=1, source_target_pairs={{0,4},{4,8},{8,12},{1,5},{5,9},{9,13},{2,6},{6,10},{10,14},{3,7},{... | collective-permute-start | bytes 12296 | tf_op jit(solution)/shard_map/ppermute | solution.py:12
  11.4 3.7 %copy-start.19 = (f32[32,64]{1,0:T(8,128)S(1)}, f32[32,64]{1,0:T(8,128)}, u32[]{:S(2)}) copy-start(f32[32,64]{1,0:T(8,128)} %param.14) | copy-start | bytes 24580
  11.4 3.7 %copy-start.20 = (f32[32,64]{1,0:T(8,128)S(1)}, f32[32,64]{1,0:T(8,128)}, u32[]{:S(2)}) copy-start(f32[32,64]{1,0:T(8,128)} %param.15) | copy-start | bytes 24580
  11.4 5.7 %copy-start.29 = (bf16[1024]{0:T(1024)(128)(2,1)S(1)}, bf16[1024]{0:T(1024)(128)(2,1)}, u32[]{:S(2)}) copy-start(bf16[1024]{0:T(1024)(128)(2,1)} %param.11) | copy-start | bytes 6148
  15.0 6.9 %copy-start.21 = (f32[3,3,512]{2,1,0:T(4,128)S(1)}, f32[3,3,512]{2,1,0:T(4,128)}, u32[]{:S(2)}) copy-start(f32[3,3,512]{2,1,0:T(4,128)} %param.13) | copy-start | bytes 55300
  15.7 3.3 %copy-start.18 = (f32[32,64]{1,0:T(8,128)}, f32[32,64]{1,0:T(8,128)S(1)}, u32[]{:S(2)}) copy-start(f32[32,64]{1,0:T(8,128)S(1)} %get-tuple-element.112) | copy-start | bytes 24580
  18.2 29.7 %collective-permute-start.1 = (bf16[387,1024]{1,0:T(8,128)(2,1)}, bf16[387,1024]{1,0:T(8,128)(2,1)S(1)}, u32[]{:S(2)}, u32[]{:S(2)}) collective-permute-start(bf16[387,1024]{1,0:T(8,128)(2,1)} %pad_maximum_fusion.2), channel_id=1, source_target_pairs={{0,3},{1,0},{2,1},{3,2},{4,7},{5,4},{6,5},{7,6},{8,11},{9,8},{10,9... | collective-permute-start | bytes 2377736 | tf_op jit(solution)/shard_map/ppermute | solution.py:38
  20.7 27.4 %collective-permute-start.2 = (bf16[387,1024]{1,0:T(8,128)(2,1)}, bf16[387,1024]{1,0:T(8,128)(2,1)S(1)}, u32[]{:S(2)}, u32[]{:S(2)}) collective-permute-start(bf16[387,1024]{1,0:T(8,128)(2,1)} %pad_maximum_fusion.2), channel_id=1, source_target_pairs={{0,2},{1,3},{2,0},{3,1},{4,6},{5,7},{6,4},{7,5},{8,10},{9,11},{10,... | collective-permute-start | bytes 2377736 | tf_op jit(solution)/shard_map/ppermute | solution.py:38
  22.5 32.8 %collective-permute-start.3 = (bf16[387,1024]{1,0:T(8,128)(2,1)}, bf16[387,1024]{1,0:T(8,128)(2,1)S(1)}, u32[]{:S(2)}, u32[]{:S(2)}) collective-permute-start(bf16[387,1024]{1,0:T(8,128)(2,1)} %pad_maximum_fusion.2), channel_id=1, source_target_pairs={{0,1},{1,2},{2,3},{3,0},{4,5},{5,6},{6,7},{7,4},{8,9},{9,10},{10,1... | collective-permute-start | bytes 2377736 | tf_op jit(solution)/shard_map/ppermute | solution.py:38
  77.9 84.3 %copy-start.4 = (bf16[386,4,512]{2,0,1:T(8,128)(2,1)}, bf16[386,4,512]{2,0,1:T(8,128)(2,1)S(1)}, u32[]{:S(2)}) copy-start(bf16[386,4,512]{2,0,1:T(8,128)(2,1)S(1)} %fusion.5) | copy-start | bytes 4743172
  80.5 79.4 %collective-permute-start.5 = (bf16[3,512,512]{2,1,0:T(8,128)(2,1)S(1)}, bf16[3,512,512]{2,1,0:T(8,128)(2,1)}, u32[]{:S(2)}, u32[]{:S(2)}) collective-permute-start(bf16[3,512,512]{2,1,0:T(8,128)(2,1)S(1)} %fusion.7), channel_id=1, source_target_pairs={{0,16},{16,0},{1,17},{17,1},{2,18},{18,2},{3,19},{19,3},{4,20},{20... | collective-permute-start | bytes 4718600 | tf_op jit(solution)/shard_map/ppermute | solution.py:105
  103.4 58.7 %collective-permute-start.6 = (bf16[3,512,512]{2,1,0:T(8,128)(2,1)}, bf16[3,512,512]{2,1,0:T(8,128)(2,1)}, u32[]{:S(2)}, u32[]{:S(2)}) collective-permute-start(bf16[3,512,512]{2,1,0:T(8,128)(2,1)} %fusion.6), channel_id=1, source_target_pairs={{0,16},{16,0},{1,17},{17,1},{2,18},{18,2},{3,19},{19,3},{4,20},{20... | collective-permute-start | bytes 4718600 | tf_op jit(solution)/shard_map/ppermute | solution.py:105
  146.3 4.2 %copy-start.8 = (bf16[386,4,1,512]{3,2,1,0:T(2,128)(2,1)S(1)}, bf16[386,4,1,512]{3,2,1,0:T(2,128)(2,1)}, u32[]{:S(2)}) copy-start(bf16[386,4,1,512]{3,2,1,0:T(2,128)(2,1)} %get-tuple-element.90) | copy-start | bytes 4743172
  149.6 52.5 %collective-permute-start.4 = (bf16[3,512,512]{2,1,0:T(8,128)(2,1)}, bf16[3,512,512]{2,1,0:T(8,128)(2,1)}, u32[]{:S(2)}, u32[]{:S(2)}) collective-permute-start(bf16[3,512,512]{2,1,0:T(8,128)(2,1)} %fusion.8), channel_id=1, source_target_pairs={{0,16},{16,0},{1,17},{17,1},{2,18},{18,2},{3,19},{19,3},{4,20},{20... | collective-permute-start | bytes 4718600 | tf_op jit(solution)/shard_map/ppermute | solution.py:105
  150.5 2.8 %copy-start.11 = (bf16[1024,1,512]{2,0,1:T(8,128)(2,1)S(1)}, bf16[1024,1,512]{2,0,1:T(8,128)(2,1)}, u32[]{:S(2)}) copy-start(bf16[1024,1,512]{2,0,1:T(8,128)(2,1)} %get-tuple-element.93) | copy-start | bytes 3145732
  167.9 6.9 %copy-start.9 = (bf16[1024,1,512]{2,0,1:T(8,128)(2,1)S(1)}, bf16[1024,1,512]{2,0,1:T(8,128)(2,1)}, u32[]{:S(2)}) copy-start(bf16[1024,1,512]{2,0,1:T(8,128)(2,1)} %get-tuple-element.91) | copy-start | bytes 3145732
  170.5 26.3 %copy-start.15 = (f32[32,64]{1,0:T(8,128)S(1)}, f32[32,64]{1,0:T(8,128)}, u32[]{:S(2)}) copy-start(f32[32,64]{1,0:T(8,128)} %get-tuple-element.107) | copy-start | bytes 24580
  170.5 26.3 %copy-start.16 = (f32[32,64]{1,0:T(8,128)S(1)}, f32[32,64]{1,0:T(8,128)}, u32[]{:S(2)}) copy-start(f32[32,64]{1,0:T(8,128)} %get-tuple-element.108) | copy-start | bytes 24580
  170.5 26.3 %copy-start.17 = (f32[32,64]{1,0:T(8,128)S(1)}, f32[32,64]{1,0:T(8,128)}, u32[]{:S(2)}) copy-start(f32[32,64]{1,0:T(8,128)} %get-tuple-element.109) | copy-start | bytes 24580
  170.5 26.4 %copy-start.7 = (f32[32,128,64]{1,2,0:T(8,128)S(1)}, f32[32,128,64]{1,2,0:T(8,128)}, u32[]{:S(2)}) copy-start(f32[32,128,64]{1,2,0:T(8,128)} %exponential_multiply_fusion) | copy-start | bytes 3145732
  170.5 26.4 %copy-start.14 = (f32[3,32,64,16]{2,3,1,0:T(8,128)S(1)}, f32[3,32,64,16]{2,3,1,0:T(8,128)}, u32[]{:S(2)}) copy-start(f32[3,32,64,16]{2,3,1,0:T(8,128)} %get-tuple-element.43) | copy-start | bytes 1179652
  170.5 9.2 %collective-permute-start.7 = (f32[32,64,16]{1,2,0:T(8,128)S(1)}, f32[32,64,16]{1,2,0:T(8,128)S(1)}, u32[]{:S(2)}, u32[]{:S(2)}) collective-permute-start(f32[32,64,16]{1,2,0:T(8,128)S(1)} %get-tuple-element.42), channel_id=1, source_target_pairs={{0,4},{4,8},{8,12},{1,5},{5,9},{9,13},{2,6},{6,10},{10,14},{3,7},{... | collective-permute-start | bytes 393224 | tf_op jit(solution)/shard_map/ppermute | solution.py:153
  172.0 24.8 %collective-permute-start.8 = (f32[32,64,16]{1,2,0:T(8,128)S(1)}, f32[32,64,16]{1,2,0:T(8,128)S(1)}, u32[]{:S(2)}, u32[]{:S(2)}) collective-permute-start(f32[32,64,16]{1,2,0:T(8,128)S(1)} %get-tuple-element.42), channel_id=1, source_target_pairs={{0,8},{4,12},{1,9},{5,13},{2,10},{6,14},{3,11},{7,15},{16,24},{20,... | collective-permute-start | bytes 393224 | tf_op jit(solution)/shard_map/ppermute | solution.py:153
  173.3 23.5 %collective-permute-start.9 = (f32[32,64,16]{1,2,0:T(8,128)S(1)}, f32[32,64,16]{1,2,0:T(8,128)S(1)}, u32[]{:S(2)}, u32[]{:S(2)}) collective-permute-start(f32[32,64,16]{1,2,0:T(8,128)S(1)} %get-tuple-element.42), channel_id=1, source_target_pairs={{0,12},{1,13},{2,14},{3,15},{16,28},{17,29},{18,30},{19,31}} | collective-permute-start | bytes 393224 | tf_op jit(solution)/shard_map/ppermute | solution.py:153
  177.4 20.8 %copy-start.1 = (f32[32,128,128]{2,1,0:T(8,128)S(1)}, f32[32,128,128]{2,1,0:T(8,128)}, u32[]{:S(2)}) copy-start(f32[32,128,128]{2,1,0:T(8,128)} %slice.156) | copy-start | bytes 6291460
  205.8 12.1 %copy-start = (s32[4]{0:T(128)S(1)}, s32[4]{0:T(128)}, u32[]{:S(2)}) copy-start(s32[4]{0:T(128)} %constant.143.clone) | copy-start | bytes 52
  206.1 8.8 %collective-permute-start.10 = (bf16[1,384,512]{2,1,0:T(8,128)(2,1)S(1)}, bf16[1,384,512]{2,1,0:T(8,128)(2,1)S(1)}, u32[]{:S(2)}, u32[]{:S(2)}) collective-permute-start(bf16[1,384,512]{2,1,0:T(8,128)(2,1)S(1)} %fusion.54), channel_id=1, source_target_pairs={{0,2},{1,3},{2,0},{3,1},{4,6},{5,7},{6,4},{7,5},{8,10},{9,11},{10,... | collective-permute-start | bytes 1179656 | tf_op jit(solution)/shard_map/ppermute | solution.py:57
  215.0 4.8 %collective-permute-start.11 = (bf16[2,384,512]{2,1,0:T(8,128)(2,1)S(1)}, bf16[2,384,512]{2,1,0:T(8,128)(2,1)S(1)}, u32[]{:S(2)}, u32[]{:S(2)}) collective-permute-start(bf16[2,384,512]{2,1,0:T(8,128)(2,1)S(1)} %pad_maximum_fusion.3), channel_id=1, source_target_pairs={{0,1},{1,0},{2,3},{3,2},{4,5},{5,4},{6,7},{7,6},{8,9},{9,8},{10,11... | collective-permute-start | bytes 2359304 | tf_op jit(solution)/shard_map/ppermute | solution.py:57
  (13 other events, 25.2 us)
Sparse Core Ops, SparseCore 0:
  9.3 44.8 all-gather.8
  55.8 44.4 all-gather.10
  101.9 44.4 all-gather.6
